TPU v7x, 32 devices: a whole 2x2x4 slice. The times are simulated.
32 devices in a mesh: case: 2 (over y), tm: 4 (over z), bundle: 2 (over x), sub: 2 (over core).
Axes of the slice: x: 2, y: 2, z: 4, core: 2. Of those that a mesh axis runs over, the one named last changes fastest.
Arguments:
- cotangent: bfloat16 [16384, 512], P(('case', 'tm'), 'bundle'), parts along dimension 0, may hold values from -28 to 28
- inputs: bfloat16 [16384, 512], P(('case', 'tm'), 'bundle'), parts along dimension 0, may hold values from -6 to 6
- impulse: bfloat16 [8, 128, 4096], P('bundle', 'sub'), may hold values from -0.0625 to 0.0625
- terminal: int32 [8, 64], P('bundle'), may hold values from 0 to 63, each once within a row
- fault_step: int32 [2], P('case'), parts along dimension 0, may hold values from 0 to 4095
Outputs:
- voltage_grad: bfloat16 [16384, 512], P(('case', 'tm', 'sub'), 'bundle'), parts along dimension 0
- impulse_grad: float32 [16, 128, 4096], P(('case', 'bundle'), 'sub', 'tm'), parts along dimension 0
There are 2 independent parts, one for each index of `case`. A program takes and returns all parts, laid end to end along the dimension named above; an argument that names none is the same for every part. Nothing has to cross between parts.
Inputs may be any that keep to these rules, and one draw needn't show every extreme that they name: Each row of terminal orders the 64 terminals of a bundle, each once.
All inputs are finite; a program needn't handle non-finite values.
Results may differ from a plain program's by a relative error of at most 0.001.
Values may be sent and summed in bfloat16 or wider, within the bound.
No kernel may reach another device: no remote copies, remote signals or barrier semaphores. Data moves between devices by JAX's collectives and lax.ppermute only.
A program may use at most 320 MiB of HBM per device.

v0:
```python
import math

import jax
import jax.numpy as jnp
from jax import lax
from jax.sharding import PartitionSpec as P

CB = 64
NB = 8
L = 128


norm_ratio = 0.5
tile_rows = 8


def passed_along(block, axis, distance):
    devices = range(lax.axis_size(axis))
    route = [(i - distance, i) for i in devices if i - distance in devices]
    return lax.ppermute(block, axis, route)


def tiles_of(source, start, block_rows, lag_count):
    bundles = source.shape[0]
    width = source.shape[2]
    window = lax.dynamic_slice_in_dim(source, start, block_rows + lag_count, 1)
    tiled = window.reshape(bundles, (block_rows + lag_count) // tile_rows, tile_rows, width)
    tile_count = block_rows // tile_rows
    spans = [tiled[:, first : first + tile_count] for first in range(lag_count // tile_rows + 1)]
    wide = jnp.concatenate(spans, axis=2)
    return wide.reshape(bundles, tile_count, (lag_count + tile_rows) * width)


def local(cotangent, inputs, impulse, terminal, fault_step):
    seg_rows = cotangent.shape[0]
    local_bundles = terminal.shape[0]
    bundle_width = terminal.shape[1]
    lag_count = impulse.shape[1]
    all_lags = lag_count * lax.axis_size("sub")
    lag_first = lax.axis_index("sub") * lag_count
    columns = jnp.arange(bundle_width, dtype=jnp.int32)
    onehot = (terminal[:, :, None] == columns[None, None, :]).astype(jnp.bfloat16)
    grad_in = cotangent.reshape(seg_rows, local_bundles, bundle_width)
    reordered = jnp.einsum(
        "tbi,bir->tbr", grad_in, onehot, preferred_element_type=jnp.float32
    ).astype(jnp.bfloat16)
    seg_start = lax.axis_index("tm") * seg_rows
    steps_here = seg_start + jnp.arange(seg_rows, dtype=jnp.int32)
    live_rows = steps_here >= fault_step[0]
    masked = jnp.where(
        live_rows[:, None, None],
        inputs.reshape(seg_rows, local_bundles, bundle_width),
        jnp.zeros((), jnp.bfloat16),
    )
    ahead_rows = passed_along(reordered[:all_lags], "tm", -1)
    extended = jnp.concatenate([reordered, ahead_rows], axis=0)
    ext_lanes = jnp.transpose(extended, (1, 0, 2))
    reord_lanes = jnp.transpose(reordered, (1, 0, 2))
    kernel = impulse.reshape(local_bundles, lag_count, bundle_width, bundle_width)
    zero_pad = jnp.zeros((local_bundles, tile_rows, bundle_width, bundle_width), jnp.bfloat16)
    kernel_pad = jnp.concatenate([zero_pad, kernel, zero_pad], axis=1)
    toeplitz = jnp.stack(
        [
            kernel_pad[:, tile_rows - shift_row : tile_rows - shift_row + lag_count + tile_rows]
            for shift_row in range(tile_rows)
        ],
        axis=3,
    )
    toeplitz = toeplitz.reshape(
        local_bundles, (lag_count + tile_rows) * bundle_width, tile_rows * bundle_width
    )
    block_rows = min(512, seg_rows)
    block_count = seg_rows // block_rows
    tile_count = block_rows // tile_rows
    behind = passed_along(masked[seg_rows - all_lags :], "tm", 1)
    history = jnp.concatenate([behind, masked], axis=0)
    hist_lanes = jnp.transpose(history, (1, 0, 2))

    def advance(grad_acc, block_index):
        row_start = block_index * block_rows
        wide = tiles_of(ext_lanes, row_start + lag_first, block_rows, lag_count)
        dx_block = jnp.einsum("bkx,bxy->bky", wide, toeplitz, preferred_element_type=jnp.float32)
        row_block = lax.dynamic_slice_in_dim(reord_lanes, row_start, block_rows, 1).reshape(
            local_bundles, tile_count, tile_rows * bundle_width
        )
        earlier = tiles_of(
            hist_lanes, row_start + all_lags - lag_first - lag_count, block_rows, lag_count
        )
        grad_acc = grad_acc + jnp.einsum(
            "bkx,bky->bxy", row_block, earlier, preferred_element_type=jnp.float32
        )
        return (grad_acc, dx_block.reshape(local_bundles, block_rows, bundle_width))

    acc_shape = (local_bundles, tile_rows * bundle_width, (lag_count + tile_rows) * bundle_width)
    grad_total, dx_blocks = lax.scan(
        advance, jnp.zeros(acc_shape, jnp.float32), jnp.arange(block_count, dtype=jnp.int32)
    )
    partial_dx = jnp.transpose(dx_blocks, (0, 2, 1, 3)).reshape(
        seg_rows, local_bundles * bundle_width
    )
    folded = grad_total.reshape(
        local_bundles, tile_rows, bundle_width, lag_count + tile_rows, bundle_width
    )
    lag_sum = folded[:, 0, :, 1 : lag_count + 1, :]
    for shift_row in range(1, tile_rows):
        lag_sum = lag_sum + folded[:, shift_row, :, shift_row + 1 : shift_row + lag_count + 1, :]
    grad_blocks = jnp.transpose(jnp.flip(lag_sum, axis=2), (0, 2, 1, 3))
    summed_dx = lax.psum_scatter(partial_dx, "sub", scatter_dimension=0, tiled=True)
    share_rows = summed_dx.shape[0]
    own_steps = (
        seg_start + lax.axis_index("sub") * share_rows + jnp.arange(share_rows, dtype=jnp.int32)
    )
    voltage_grad = jnp.where((own_steps >= fault_step[0])[:, None], summed_dx, 0.0).astype(
        jnp.bfloat16
    )
    grad_flat = grad_blocks.reshape(local_bundles, lag_count, bundle_width * bundle_width)
    grad_sum = lax.psum(grad_flat, "tm")
    share_cols = grad_flat.shape[2] // lax.axis_size("tm")
    own_grad = lax.dynamic_slice_in_dim(grad_sum, lax.axis_index("tm") * share_cols, share_cols, 2)
    own_squares = jnp.sum(own_grad * own_grad)
    total_squares = lax.psum(own_squares, ("tm", "bundle", "sub"))
    norm_limit = norm_ratio * math.sqrt(NB * L * CB * CB)
    factor = norm_limit / jnp.sqrt(total_squares + 1e-06)
    return (voltage_grad, own_grad * factor)


def solution(mesh):
    placed = (
        P(("case", "tm"), "bundle"),
        P(("case", "tm"), "bundle"),
        P("bundle", "sub", None),
        P("bundle", None),
        P("case"),
    )
    return jax.shard_map(
        local,
        mesh=mesh,
        in_specs=placed,
        out_specs=(P(("case", "tm", "sub"), "bundle"), P(("case", "bundle"), "sub", "tm")),
        check_vma=False,
    )
```

profile of v0, /device:TPU:0, one launch (start us, length us, event | category | flops | bytes accessed | tf_op | source)
XLA Modules:
  0.0 749.6 jit_solution(2607385197991196513)
XLA Ops:
  59.8 47.4 %copy.50 = bf16[4,72,64,8,64]{4,3,2,1,0:T(8,128)(2,1)} copy(bf16[4,72,64,8,64]{1,4,3,2,0:T(8,128)(2,1)} %fusion.1) | data formatting | bytes 37748736 | tf_op jit(solution)/shard_map/stack | solution.py:62
  107.2 49.1 %reshape.92 = bf16[4,4608,512]{2,1,0:T(8,128)(2,1)} reshape(bf16[4,72,64,8,64]{4,3,2,1,0:T(8,128)(2,1)} %copy.50) | data formatting | bytes 37748736 | tf_op jit(solution)/shard_map/reshape | solution.py:69
  159.7 269.9 %while.17 = (s32[]{:T(128)}, f32[4,512,4608]{2,1,0:T(8,128)}, f32[4,4,512,64]{3,2,1,0:T(8,128)}, s32[4]{0:T(128)S(1)}, bf16[4,2048,64]{1,2,0:T(8,128)(2,1)}, /*i...) while((s32[]{:T(128)}, f32[4,512,4608]{2,1,0:T(8,128)}, ...), condition=%wide.region_1.2_spmd.clone, body=%wide.region_0.1_spmd.clone.sunk | while | flops 2434793472 | bytes 131072384 | solution.py:95
  173.4 6.1 reshape.109
  179.5 8.1 %fusion.24 = f32[4,64,512]{2,1,0:T(8,128)S(1)} fusion(bf16[4,64,4608]{2,1,0:T(8,128)(2,1)S(1)} %reshape.109, bf16[4,4608,512]{2,1,0:T(8,128)(2,1)} %get-tuple-element.366), kind=kOutput, calls=%fused_computation.58.clone.1 | convolution fusion | flops 1207959552 | bytes 21757952 | tf_op jit(solution)/shard_map/while/body/eval_jaxpr/bkx,bxy->bky/dot_general | solution.py:82
  196.9 6.1 reshape.108
  203.1 14.0 %select_add_fusion.2 = f32[4,512,4608]{2,1,0:T(8,128)} fusion(f32[4,512,4608]{2,1,0:T(8,128)} %get-tuple-element.342, pred[]{:T(512)S(6)} %compare.4, bf16[4,64,512]{2,1,0:T(8,128)(2,1)S(1)} %copy-done.1, bf16[4,64,4608]{2,1,0:T(8,128)(2,1)S(1)} %reshape.108), kind=kOutput, calls=%fused_computation.clone.1 | convolution fusion | flops 1226833920 | bytes 78118912 | tf_op jit(solution)/shard_map/while/body/eval_jaxpr/bkx,bky->bxy/dot_general | solution.py:89
  230.8 6.1 reshape.109
  236.9 8.1 %fusion.24 = f32[4,64,512]{2,1,0:T(8,128)S(1)} fusion(bf16[4,64,4608]{2,1,0:T(8,128)(2,1)S(1)} %reshape.109, bf16[4,4608,512]{2,1,0:T(8,128)(2,1)} %get-tuple-element.366), kind=kOutput, calls=%fused_computation.58.clone.1 | convolution fusion | flops 1207959552 | bytes 21757952 | tf_op jit(solution)/shard_map/while/body/eval_jaxpr/bkx,bxy->bky/dot_general | solution.py:82
  254.4 6.1 reshape.108
  260.5 27.4 %select_add_fusion.2 = f32[4,512,4608]{2,1,0:T(8,128)} fusion(f32[4,512,4608]{2,1,0:T(8,128)} %get-tuple-element.342, pred[]{:T(512)S(6)} %compare.4, bf16[4,64,512]{2,1,0:T(8,128)(2,1)S(1)} %copy-done.1, bf16[4,64,4608]{2,1,0:T(8,128)(2,1)S(1)} %reshape.108), kind=kOutput, calls=%fused_computation.clone.1 | convolution fusion | flops 1226833920 | bytes 78118912 | tf_op jit(solution)/shard_map/while/body/eval_jaxpr/bkx,bky->bxy/dot_general | solution.py:89
  301.6 6.1 reshape.109
  307.8 8.1 %fusion.24 = f32[4,64,512]{2,1,0:T(8,128)S(1)} fusion(bf16[4,64,4608]{2,1,0:T(8,128)(2,1)S(1)} %reshape.109, bf16[4,4608,512]{2,1,0:T(8,128)(2,1)} %get-tuple-element.366), kind=kOutput, calls=%fused_computation.58.clone.1 | convolution fusion | flops 1207959552 | bytes 21757952 | tf_op jit(solution)/shard_map/while/body/eval_jaxpr/bkx,bxy->bky/dot_general | solution.py:82
  325.2 6.1 reshape.108
  331.4 27.4 %select_add_fusion.2 = f32[4,512,4608]{2,1,0:T(8,128)} fusion(f32[4,512,4608]{2,1,0:T(8,128)} %get-tuple-element.342, pred[]{:T(512)S(6)} %compare.4, bf16[4,64,512]{2,1,0:T(8,128)(2,1)S(1)} %copy-done.1, bf16[4,64,4608]{2,1,0:T(8,128)(2,1)S(1)} %reshape.108), kind=kOutput, calls=%fused_computation.clone.1 | convolution fusion | flops 1226833920 | bytes 78118912 | tf_op jit(solution)/shard_map/while/body/eval_jaxpr/bkx,bky->bxy/dot_general | solution.py:89
  378.6 8.1 %fusion.24 = f32[4,64,512]{2,1,0:T(8,128)S(1)} fusion(bf16[4,64,4608]{2,1,0:T(8,128)(2,1)S(1)} %reshape.109, bf16[4,4608,512]{2,1,0:T(8,128)(2,1)} %get-tuple-element.366), kind=kOutput, calls=%fused_computation.58.clone.1 | convolution fusion | flops 1207959552 | bytes 21757952 | tf_op jit(solution)/shard_map/while/body/eval_jaxpr/bkx,bxy->bky/dot_general | solution.py:82
  402.2 27.4 %select_add_fusion.2 = f32[4,512,4608]{2,1,0:T(8,128)} fusion(f32[4,512,4608]{2,1,0:T(8,128)} %get-tuple-element.342, pred[]{:T(512)S(6)} %compare.4, bf16[4,64,512]{2,1,0:T(8,128)(2,1)S(1)} %copy-done.1, bf16[4,64,4608]{2,1,0:T(8,128)(2,1)S(1)} %reshape.108), kind=kOutput, calls=%fused_computation.clone.1 | convolution fusion | flops 1226833920 | bytes 78118912 | tf_op jit(solution)/shard_map/while/body/eval_jaxpr/bkx,bky->bxy/dot_general | solution.py:89
  435.6 54.3 %reshape.94 = f32[4,8,64,72,64]{4,3,2,1,0:T(8,128)} reshape(f32[4,512,4608]{2,1,0:T(8,128)} %get-tuple-element.183) | data formatting | bytes 75497472 | tf_op jit(solution)/shard_map/reshape | solution.py:101
  489.9 27.4 %fusion = f32[4,64,64,64]{3,2,1,0:T(8,128)} fusion(f32[4,8,64,72,64]{4,3,2,1,0:T(8,128)} %reshape.94), kind=kLoop, calls=%fused_computation.24 | loop fusion | flops 7340032 | bytes 37748736 | tf_op jit(solution)/shard_map/add | solution.py:106
  517.3 11.9 %rev.4 = f32[4,64,64,64]{3,2,1,0:T(8,128)} reverse(f32[4,64,64,64]{3,2,1,0:T(8,128)} %fusion), dimensions={2} | reverse | bytes 8388608 | tf_op jit(solution)/shard_map/jit(_flip)/rev | solution.py:107
  529.1 11.5 %copy.55 = f32[4,64,64,64]{3,2,1,0:T(8,128)} copy(f32[4,64,64,64]{3,1,2,0:T(8,128)} %bitcast.113) | data formatting | bytes 8388608 | tf_op jit(solution)/shard_map/transpose | solution.py:107
  540.6 7.9 %reshape.95 = f32[4,64,4096]{2,1,0:T(8,128)} reshape(f32[4,64,64,64]{3,2,1,0:T(8,128)} %copy.55) | data formatting | bytes 8388608 | tf_op jit(solution)/shard_map/reshape | solution.py:116
  549.9 154.3 %all-reduce.3.cloned.1.call-done = f32[4,64,4096]{2,1,0:T(8,128)} async-done(((f32[4,64,4096]{2,1,0:T(8,128)}), f32[4,64,4096]{2,1,0:T(8,128)}) %all-reduce.3.cloned.1.call-update) | async-done | bytes 4194320 | tf_op jit(solution)/shard_map/psum | solution.py:117
  707.3 31.9 %psum.15 = f32[]{:T(128)} all-reduce(f32[]{:T(128)} %multiply_reduce_fusion), channel_id=1, replica_groups=mesh['case'=2,'tm'=4,'bundle'=2,'sub'=2] {'tm','bundle','sub'}, use_global_device_ids=true, to_apply=%region_5.6 | all-reduce | flops 1 | bytes 8 | tf_op jit(solution)/shard_map/psum | solution.py:121
  (161 shorter events, 168.4 us)
Async XLA Ops:
  8.0 6.5 copy-start.2
  8.0 540.5 %reduce-scatter.2.cloned.1.call-start = ((), (), s32[]{:S(2)}) async-start(), calls=%async_computation.1 | async-start | bytes 3145728 | tf_op jit(solution)/shard_map/reduce_scatter | solution.py:108
  12.5 143.7 %collective-permute-start.1 = (bf16[128,4,64]{0,2,1:T(8,128)(2,1)S(1)}, bf16[128,4,64]{0,2,1:T(8,128)(2,1)S(1)}, u32[]{:S(2)}, u32[]{:S(2)}) collective-permute-start(bf16[128,4,64]{0,2,1:T(8,128)(2,1)S(1)} %slice.269), channel_id=1, source_target_pairs={{4,0},{8,4},{12,8},{5,1},{9,5},{13,9},{6,2},{10,6},{14,10},{7,3},{... | collective-permute-start | bytes 196616 | tf_op jit(solution)/shard_map/ppermute | solution.py:20
  15.3 143.3 %collective-permute-start = (bf16[128,4,64]{0,2,1:T(8,128)(2,1)S(1)}, bf16[128,4,64]{0,2,1:T(8,128)(2,1)S(1)}, u32[]{:S(2)}, u32[]{:S(2)}) collective-permute-start(bf16[128,4,64]{0,2,1:T(8,128)(2,1)S(1)} %slice.268), channel_id=1, source_target_pairs={{0,4},{4,8},{8,12},{1,5},{5,9},{9,13},{2,6},{6,10},{10,14},{3,7},{... | collective-permute-start | bytes 196616 | tf_op jit(solution)/shard_map/ppermute | solution.py:20
  25.6 7.2 copy-start
  195.2 7.9 %copy-start.1 = (bf16[4,64,512]{2,1,0:T(8,128)(2,1)S(1)}, bf16[4,64,512]{2,1,0:T(8,128)(2,1)}, u32[]{:S(2)}) copy-start(bf16[4,64,512]{2,1,0:T(8,128)(2,1)} %reshape.107) | copy-start | bytes 786436 | tf_op jit(solution)/shard_map/while
  252.6 7.9 %copy-start.1 = (bf16[4,64,512]{2,1,0:T(8,128)(2,1)S(1)}, bf16[4,64,512]{2,1,0:T(8,128)(2,1)}, u32[]{:S(2)}) copy-start(bf16[4,64,512]{2,1,0:T(8,128)(2,1)} %reshape.107) | copy-start | bytes 786436 | tf_op jit(solution)/shard_map/while
  323.4 7.9 %copy-start.1 = (bf16[4,64,512]{2,1,0:T(8,128)(2,1)S(1)}, bf16[4,64,512]{2,1,0:T(8,128)(2,1)}, u32[]{:S(2)}) copy-start(bf16[4,64,512]{2,1,0:T(8,128)(2,1)} %reshape.107) | copy-start | bytes 786436 | tf_op jit(solution)/shard_map/while
  394.2 7.9 %copy-start.1 = (bf16[4,64,512]{2,1,0:T(8,128)(2,1)S(1)}, bf16[4,64,512]{2,1,0:T(8,128)(2,1)}, u32[]{:S(2)}) copy-start(bf16[4,64,512]{2,1,0:T(8,128)(2,1)} %reshape.107) | copy-start | bytes 786436 | tf_op jit(solution)/shard_map/while
  435.5 268.7 %all-reduce.3.cloned.1.call-start = ((), (), s32[]{:S(2)}) async-start(), calls=%async_computation.2 | async-start | bytes 8388608 | tf_op jit(solution)/shard_map/psum | solution.py:117
Sparse Core Ops, SparseCore 0:
  435.7 10.2 reduce-scatter.1
Sparse Core Ops, SparseCore 1:
  548.6 155.6 all-reduce.2
where the time goes:
time: 755 us; the launch traced here: 750 us
  local copies, waits for them, and re-layouts  365 us (48%)
  waiting for transfers between devices  154 us (20%)
  matrix products  131 us (17%)
  other arithmetic  40.7 us (5%)
  blocking collectives  31.9 us (4%)
  between operations  17 us (2%)
    psum x1, waiting for transfers between devices, local(): grad_sum = lax.psum(grad_flat, 'tm')  154 us
    dot_general x4, matrix products, advance(): jnp.einsum('bkx,bky->bxy', row_block, earlier, preferred_element_type=jnp...  96.3 us
    while x72, local copies, waits for them, and re-layouts  56.9 us
    reshape x1, local copies, waits for them, and re-layouts, local(): grad_total.reshape(local_bundles, tile_rows, bundle_width, lag_count + ti...  54.3 us
    another operation x2, local copies, waits for them, and re-layouts, local(): jnp.stack([kernel_pad[:, tile_rows - shift_row:tile_rows - shift_row + la...  50.8 us
    reshape x8, local copies, waits for them, and re-layouts, tiles_of(): return wide.reshape(bundles, tile_count, (lag_count + tile_rows) * width)  49.2 us
    reshape x1, local copies, waits for them, and re-layouts, local(): toeplitz.reshape(local_bundles, (lag_count + tile_rows) * bundle_width, t...  49.1 us
    unnamed x16, local copies, waits for them, and re-layouts  35.8 us
  transfers between devices with their start and end apart: 4, of which 1 were waited for; matrix products, arithmetic and copies ran while one was open for 34% of the time, Pallas kernels for 0%

commit v1 on v0

v1 whole, which is shorter than its diff:
```python
import functools
import math

import jax
import jax.numpy as jnp
from jax import lax
from jax.experimental import pallas as pl
from jax.sharding import PartitionSpec as P

CB = 64
NB = 8
L = 128


norm_ratio = 0.5
tile_rows = 4
chunk_rows = 256
_INTERPRET = False


def passed_along(block, axis, distance):
    devices = range(lax.axis_size(axis))
    route = [(i - distance, i) for i in devices if i - distance in devices]
    return lax.ppermute(block, axis, route)


def dx_kernel(r_ref, t_ref, o_ref, *, lag_tiles, rows):
    width = o_ref.shape[2]
    for c in range(rows // chunk_rows):
        base = c * chunk_rows
        acc = jnp.zeros((chunk_rows, width), jnp.float32)
        for q in range(lag_tiles):
            x = r_ref[0, base + q : base + q + chunk_rows, :].astype(jnp.bfloat16)
            acc = acc + jnp.dot(x, t_ref[0, q], preferred_element_type=jnp.float32)
        o_ref[0, base : base + chunk_rows, :] = acc


def raw_kernel(rt_ref, m_ref, o_ref, *, shift, rows, width):
    rt = rt_ref[0]

    def corr(q):
        m = m_ref[0, shift - q : shift - q + rows, :].astype(jnp.bfloat16)
        return jnp.dot(rt, m, preferred_element_type=jnp.float32)

    g_prev = corr(0)
    for a in range(shift):
        g_next = corr(a + 1)
        for d in range(tile_rows):
            acc = None
            for s in range(tile_rows):
                u = s - d
                if 0 <= u < tile_rows:
                    blk = g_prev[s * width : (s + 1) * width, u * width : (u + 1) * width]
                    acc = blk if acc is None else acc + blk
                u = s - d + tile_rows
                if 0 <= u < tile_rows:
                    blk = g_next[s * width : (s + 1) * width, u * width : (u + 1) * width]
                    acc = blk if acc is None else acc + blk
            o_ref[0, tile_rows * a + d] = acc
        g_prev = g_next


def local(cotangent, inputs, impulse, terminal, fault_step):
    seg_rows = cotangent.shape[0]
    nb = terminal.shape[0]
    width = terminal.shape[1]
    lag_count = impulse.shape[1]
    n_sub = lax.axis_size("sub")
    sub = lax.axis_index("sub")
    all_lags = lag_count * n_sub
    tr = tile_rows
    rows4 = seg_rows // tr
    wide = tr * width
    shift = lag_count // tr
    halo = all_lags // tr
    lag_tiles = shift + 1

    columns = jnp.arange(width, dtype=jnp.int32)
    onehot = (terminal[:, :, None] == columns[None, None, :]).astype(jnp.bfloat16)
    cot4 = cotangent.reshape(rows4, tr, nb, width)
    reord4 = jnp.einsum(
        "ksbi,bir->bksr", cot4, onehot, preferred_element_type=jnp.float32
    ).astype(jnp.bfloat16)
    r4 = reord4.reshape(nb, rows4, wide)
    r4t = jnp.transpose(reord4, (0, 2, 3, 1)).reshape(nb, wide, rows4)

    seg_start = lax.axis_index("tm") * seg_rows
    steps4 = seg_start + tr * jnp.arange(rows4, dtype=jnp.int32)[:, None] + jnp.arange(tr, dtype=jnp.int32)[None, :]
    live4 = steps4 >= fault_step[0]
    inp4 = jnp.transpose(inputs.reshape(rows4, tr, nb, width), (2, 0, 1, 3))
    m4 = jnp.where(live4[None, :, :, None], inp4, jnp.zeros((), jnp.bfloat16)).reshape(nb, rows4, wide)

    ahead = passed_along(r4[:, :halo], "tm", -1)
    r4ext = jnp.concatenate([r4, ahead], axis=1).astype(jnp.float32)
    r4w = lax.dynamic_slice_in_dim(r4ext, sub * shift, rows4 + shift, 1)
    behind = passed_along(m4[:, rows4 - halo :], "tm", 1)
    m4ext = jnp.concatenate([behind, m4], axis=1).astype(jnp.float32)
    m4w = lax.dynamic_slice_in_dim(m4ext, (n_sub - 1 - sub) * shift, rows4 + shift, 1)

    kern = impulse.reshape(nb, lag_count, width, width)
    kpad = jnp.pad(kern, ((0, 0), (tr - 1, tr), (0, 0), (0, 0)))
    rows_of = []
    for s in range(tr):
        cols_of = []
        for u in range(tr):
            start = s - u + tr - 1
            cols_of.append(lax.slice_in_dim(kpad, start, start + tr * shift + 1, tr, 1))
        rows_of.append(jnp.stack(cols_of, axis=3))
    toeplitz = jnp.stack(rows_of, axis=2).reshape(nb, lag_tiles, wide, wide)

    partial_dx = pl.pallas_call(
        functools.partial(dx_kernel, lag_tiles=lag_tiles, rows=rows4),
        grid=(nb,),
        in_specs=[
            pl.BlockSpec((1, rows4 + shift, wide), lambda b: (b, 0, 0)),
            pl.BlockSpec((1, lag_tiles, wide, wide), lambda b: (b, 0, 0, 0)),
        ],
        out_specs=pl.BlockSpec((1, rows4, wide), lambda b: (b, 0, 0)),
        out_shape=jax.ShapeDtypeStruct((nb, rows4, wide), jnp.float32),
        interpret=_INTERPRET,
    )(r4w, toeplitz)

    raw = pl.pallas_call(
        functools.partial(raw_kernel, shift=shift, rows=rows4, width=width),
        grid=(nb,),
        in_specs=[
            pl.BlockSpec((1, wide, rows4), lambda b: (b, 0, 0)),
            pl.BlockSpec((1, rows4 + shift, wide), lambda b: (b, 0, 0)),
        ],
        out_specs=pl.BlockSpec((1, lag_count, width, width), lambda b: (b, 0, 0, 0)),
        out_shape=jax.ShapeDtypeStruct((nb, lag_count, width, width), jnp.float32),
        interpret=_INTERPRET,
    )(r4t, m4w)

    summed_dx = lax.psum_scatter(partial_dx, "sub", scatter_dimension=1, tiled=True)
    share4 = summed_dx.shape[1]
    own_steps = (
        seg_start
        + sub * share4 * tr
        + tr * jnp.arange(share4, dtype=jnp.int32)[:, None]
        + jnp.arange(tr, dtype=jnp.int32)[None, :]
    )
    dx = jnp.where(
        (own_steps >= fault_step[0])[None, :, :, None],
        summed_dx.reshape(nb, share4, tr, width),
        0.0,
    ).astype(jnp.bfloat16)
    voltage_grad = jnp.transpose(dx, (1, 2, 0, 3)).reshape(share4 * tr, nb * width)

    grad_flat = raw.reshape(nb, lag_count, width * width)
    own_grad = lax.psum_scatter(grad_flat, "tm", scatter_dimension=2, tiled=True)
    own_squares = jnp.sum(own_grad * own_grad)
    total_squares = lax.psum(own_squares, ("tm", "bundle", "sub"))
    norm_limit = norm_ratio * math.sqrt(NB * L * CB * CB)
    factor = norm_limit / jnp.sqrt(total_squares + 1e-06)
    return (voltage_grad, own_grad * factor)


def solution(mesh):
    placed = (
        P(("case", "tm"), "bundle"),
        P(("case", "tm"), "bundle"),
        P("bundle", "sub", None),
        P("bundle", None),
        P("case"),
    )
    return jax.shard_map(
        local,
        mesh=mesh,
        in_specs=placed,
        out_specs=(P(("case", "tm", "sub"), "bundle"), P(("case", "bundle"), "sub", "tm")),
        check_vma=False,
    )
```

time: 755 us -> 258 us (0.34)
  local copies, waits for them, and re-layouts: 365 us -> 73.3 us
  matrix products: 131 us -> 1.95 us
  waiting for transfers between devices: 154 us -> 78.5 us
  Pallas kernels: 0 us -> 17.6 us
  other arithmetic: 40.7 us -> 28.9 us
    psum x1 -> x0, waiting for transfers between devices: 154 us -> none  [local(): grad_sum = lax.psum(grad_flat, 'tm')]
    dot_general x9 -> x1, matrix products: 131 us -> 1.95 us  [local(): jnp.einsum('ksbi,bir->bksr', cot4, onehot, preferred_element_type=jnp.flo...]
    reshape x15 -> x8, local copies, waits for them, and re-layouts: 165 us -> 47.1 us  [the longest x1 25.6 us: local(): toeplitz = jnp.stack(rows_of, axis=2).reshape(nb, lag_tiles, wide, wide)]
    reduce_scatter x1 -> x2, waiting for transfers between devices: 0.02 us -> 76.8 us  [the longest x1 76.8 us: local(): lax.psum_scatter(grad_flat, 'tm', scatter_dimension=2, tiled=True)]
    while x72 -> x0, local copies, waits for them, and re-layouts: 56.9 us -> none
    unnamed x16 -> x4, local copies, waits for them, and re-layouts: 35.8 us -> 0.01 us
    another operation x2, local copies, waits for them, and re-layouts: 50.8 us -> 20.8 us  [the longest x1 16.5 us: local(): toeplitz = jnp.stack(rows_of, axis=2).reshape(nb, lag_tiles, wide, wide)]
    add x1 -> x2, other arithmetic: 27.4 us -> 0.01 us  [the longest x1 0.01 us: local(): seg_start + sub * share4 * tr]
  transfers between devices with their start and end apart: 4 -> 4, of which waited for: 1 -> 2; matrix products, arithmetic and copies ran while one was open for 34% -> 35% of each run, Pallas kernels for 0% -> 3%
where the time goes in v1:
time: 258 us; the launch traced here: 256 us
  waiting for transfers between devices  78.5 us (30%)
  local copies, waits for them, and re-layouts  73.3 us (28%)
  blocking collectives  33.2 us (13%)
  other arithmetic  28.9 us (11%)
  Pallas kernels  17.6 us (7%)
  between operations  15.6 us (6%)
  starting transfers between devices  7.14 us (3%)
    reduce_scatter x1, waiting for transfers between devices, local(): lax.psum_scatter(grad_flat, 'tm', scatter_dimension=2, tiled=True)  76.8 us
    psum x1, blocking collectives, local(): total_squares = lax.psum(own_squares, ('tm', 'bundle', 'sub'))  33.2 us
    reshape x1, local copies, waits for them, and re-layouts, local(): toeplitz = jnp.stack(rows_of, axis=2).reshape(nb, lag_tiles, wide, wide)  25.6 us
    another operation x1, local copies, waits for them, and re-layouts, local(): toeplitz = jnp.stack(rows_of, axis=2).reshape(nb, lag_tiles, wide, wide)  16.5 us
    another operation x2, other arithmetic, local(): toeplitz = jnp.stack(rows_of, axis=2).reshape(nb, lag_tiles, wide, wide)  12.7 us
    pallas_call x1, Pallas kernels, local(): pl.pallas_call(functools.partial(dx_kernel, lag_tiles=lag_tiles, rows=row...  8.8 us
    pallas_call x1, Pallas kernels, local(): pl.pallas_call(functools.partial(raw_kernel, shift=shift, rows=rows4, wid...  8.8 us
    select_n x1, other arithmetic, local(): jnp.where(live4[None, :, :, None], inp4, jnp.zeros((), jnp.bfloat16))  8.23 us
  transfers between devices with their start and end apart: 4, of which 2 were waited for; matrix products, arithmetic and copies ran while one was open for 35% of the time, Pallas kernels for 3%

profile of v1, /device:TPU:0, one launch (start us, length us, event | category | flops | bytes accessed | tf_op | source)
XLA Modules:
  0.0 256.1 jit_solution(16285009622857388869)
XLA Ops:
  7.2 3.3 %reshape.95 = bf16[512,4,4,64]{3,2,1,0:T(4,128)(2,1)S(1)} reshape(bf16[2048,256]{1,0:T(8,128)(2,1)} %param.5) | data formatting | bytes 2097152 | tf_op jit(solution)/shard_map/reshape | solution.py:80
  10.5 2.0 fusion.2
  13.1 1.3 collective-permute-start
  14.4 6.9 %reshape.97 = bf16[4,64,64,64]{3,2,1,0:T(8,128)(2,1)} reshape(bf16[4,64,4096]{2,1,0:T(8,128)(2,1)} %param.7) | data formatting | bytes 4194304 | tf_op jit(solution)/shard_map/reshape | solution.py:100
  21.2 4.3 %fusion.8 = (bf16[4,17,64,1,64]{4,2,1,0,3:T(8,128)(2,1)S(1)}, bf16[4,17,64,1,64]{4,2,1,0,3:T(8,128)(2,1)S(1)}, bf16[4,17,64,1,64]{4,2,1,0,3:T(8,128)(2,1)S(1)}, ...) fusion(bf16[4,64,64,64]{3,2,1,0:T(8,128)(2,1)} %reshape.97), kind=kLoop, calls=%fused_computation.19 | loop fusion | bytes 5996544 | tf_op jit(solution)/shard_map/stack | solution.py:108
  25.5 5.2 %maximum_bitcast_fusion = (bf16[4,17,1,64,4,64]{5,3,1,0,4,2:T(8,128)(2,1)S(1)}, bf16[4,17,1,64,4,64]{5,3,1,0,4,2:T(8,128)(2,1)S(1)}, bf16[4,17,1,64,4,64]{5,3,1,...) fusion(bf16[4,17,64,1,64]{4,2,1,0,3:T(8,128)(2,1)S(1)} %get-tuple-element.2, ...), kind=kLoop, calls=%fused_computation.1 | loop fusion | flops 13369344 | bytes 12812288 | tf_op jit(solution)/shard_map/stack | solution.py:109
  30.7 7.5 %pad_maximum_fusion = bf16[4,17,4,64,4,64]{5,3,1,0,4,2:T(8,128)(2,1)S(1)} fusion(bf16[4,17,1,64,4,64]{5,3,1,0,4,2:T(8,128)(2,1)} %get-tuple-element.12, bf16[4,17,1,64,4,64]{5,3,1,0,4,2:T(8,128)(2,1)S(1)} %get-tuple-element.11, bf16[4,17,1,64,4,64]{5,3,1,0,4,2:T(8,128)(2,1)S(1)} %get-tuple-element.10, bf16[4,17,1,64,4,64]{5,3,1,0,4,2:T(8,128)(2,1)S(1)} %get-tuple-element.9), kind=kLoop, calls=%fused_computation | loop fusion | flops 13369344 | bytes 17825792 | tf_op jit(solution)/shard_map/stack | solution.py:109
  38.2 16.5 %copy.23 = bf16[4,17,4,64,4,64]{5,4,3,2,1,0:T(4,128)(2,1)} copy(bf16[4,17,4,64,4,64]{5,3,1,0,4,2:T(8,128)(2,1)S(1)} %pad_maximum_fusion) | data formatting | bytes 17825792 | tf_op jit(solution)/shard_map/stack | solution.py:109
  54.7 25.6 %reshape.98.t_ref = bf16[4,17,256,256]{3,2,1,0:T(8,128)(2,1)} reshape(bf16[4,17,4,64,4,64]{5,4,3,2,1,0:T(4,128)(2,1)} %copy.23) | data formatting | bytes 17825792 | tf_op jit(solution)/shard_map/reshape | solution.py:109
  80.3 1.7 fusion.15.r_ref
  82.1 8.8 %shard_map.68 = f32[4,512,256]{2,1,0:T(8,128)} custom-call(f32[4,528,256]{2,1,0:T(8,128)} %fusion.15.r_ref, bf16[4,17,256,256]{3,2,1,0:T(8,128)(2,1)} %reshape.98.t_ref), custom_call_target="tpu_custom_call" | custom-call | tf_op jit(solution)/shard_map/pallas_call | solution.py:111
  92.6 8.2 %select_bitcast_fusion = bf16[4,512,4,64]{3,0,2,1:T(4,128)(2,1)} fusion(bf16[512,4,4,64]{3,2,1,0:T(4,128)(2,1)S(1)} %reshape.102, pred[512,4]{1,0:T(8,128)(4,1)S(1)} %add_compare_fusion), kind=kLoop, calls=%fused_computation.14 | loop fusion | flops 524288 | bytes 2099200 | tf_op jit(solution)/shard_map/jit(_where)/select_n | solution.py:91
  100.8 3.0 %copy.26 = bf16[4,512,4,64]{1,3,2,0:T(8,128)(2,1)S(1)} copy(bf16[4,512,4,64]{3,0,2,1:T(4,128)(2,1)} %select_bitcast_fusion) | data formatting | bytes 2097152 | tf_op jit(solution)/shard_map/jit(_where)/select_n | solution.py:91
  104.4 5.8 %collective-permute-start.1 = (bf16[4,32,256]{2,1,0:T(8,128)(2,1)S(1)}, bf16[4,32,256]{2,1,0:T(8,128)(2,1)S(1)}, u32[]{:S(2)}, u32[]{:S(2)}) collective-permute-start(bf16[4,32,256]{2,1,0:T(8,128)(2,1)S(1)} %slice.46), channel_id=1, source_target_pairs={{0,4},{4,8},{8,12},{1,5},{5,9},{9,13},{2,6},{6,10},{10,14},{3,7},{... | collective-permute-start | bytes 196616 | tf_op jit(solution)/shard_map/ppermute | solution.py:24
  110.1 1.7 collective-permute-done.1
  111.8 1.6 fusion.13.m_ref
  113.4 8.8 %shard_map.69 = f32[4,64,64,64]{3,2,1,0:T(8,128)} custom-call(bf16[4,256,512]{2,1,0:T(8,128)(2,1)} %bitcast.45, f32[4,528,256]{2,1,0:T(8,128)} %fusion.13.m_ref), custom_call_target="tpu_custom_call" | custom-call | tf_op jit(solution)/shard_map/pallas_call | solution.py:123
  122.2 7.9 %reshape.104 = f32[4,64,4096]{2,1,0:T(8,128)} reshape(f32[4,64,64,64]{3,2,1,0:T(8,128)} %shard_map.69) | data formatting | bytes 8388608 | tf_op jit(solution)/shard_map/reshape | solution.py:150
  130.2 1.4 copy.24
  132.7 76.8 %reduce-scatter.5.cloned.1.call-done = f32[4,64,1024]{2,1,0:T(8,128)} async-done(((f32[4,64,4096]{2,1,0:T(8,128)}), f32[4,64,1024]{2,1,0:T(8,128)}) %reduce-scatter.5.cloned.1.call-update) | async-done | bytes 1048592 | tf_op jit(solution)/shard_map/reduce_scatter | solution.py:151
  209.5 2.1 multiply_reduce_fusion
  211.6 1.5 reshape.100
  213.1 33.2 %psum.7 = f32[]{:T(128)} all-reduce(f32[]{:T(128)} %multiply_reduce_fusion), channel_id=1, replica_groups=mesh['case'=2,'tm'=4,'bundle'=2,'sub'=2] {'tm','bundle','sub'}, use_global_device_ids=true, to_apply=%region_3.4 | all-reduce | flops 1 | bytes 8 | tf_op jit(solution)/shard_map/psum | solution.py:153
  247.0 2.3 broadcast_multiply_fusion
  (21 shorter events, 3.3 us)
Async XLA Ops:
  7.2 123.0 %reduce-scatter.3.cloned.1.call-start = ((), (), s32[]{:S(2)}) async-start(), calls=%async_computation.2 | async-start | bytes 3145728 | tf_op jit(solution)/shard_map/reduce_scatter | solution.py:135
  12.5 8.8 %copy-start = (bf16[4,64,512,4]{2,1,3,0:T(8,128)(2,1)}, bf16[4,64,512,4]{2,1,3,0:T(8,128)(2,1)S(1)}, u32[]{:S(2)}) copy-start(bf16[4,64,512,4]{2,1,3,0:T(8,128)(2,1)S(1)} %fusion.2) | copy-start | bytes 3145732
  13.1 67.3 %collective-permute-start = (bf16[4,32,256]{2,1,0:T(8,128)(2,1)S(1)}, bf16[4,32,256]{2,1,0:T(8,128)(2,1)S(1)}, u32[]{:S(2)}, u32[]{:S(2)}) collective-permute-start(bf16[4,32,256]{2,1,0:T(8,128)(2,1)S(1)} %slice.45), channel_id=1, source_target_pairs={{4,0},{8,4},{12,8},{5,1},{9,5},{13,9},{6,2},{10,6},{14,10},{7,3},{... | collective-permute-start | bytes 196616 | tf_op jit(solution)/shard_map/ppermute | solution.py:24
  82.1 9.5 %copy-start.1 = (bf16[2048,256]{1,0:T(8,128)(2,1)S(1)}, bf16[2048,256]{1,0:T(8,128)(2,1)}, u32[]{:S(2)}) copy-start(bf16[2048,256]{1,0:T(8,128)(2,1)} %param.6) | copy-start | bytes 3145732
  90.9 118.6 %reduce-scatter.5.cloned.1.call-start = ((), (), s32[]{:S(2)}) async-start(), calls=%async_computation.3 | async-start | bytes 5242880 | tf_op jit(solution)/shard_map/reduce_scatter | solution.py:151
  104.4 7.5 %collective-permute-start.1 = (bf16[4,32,256]{2,1,0:T(8,128)(2,1)S(1)}, bf16[4,32,256]{2,1,0:T(8,128)(2,1)S(1)}, u32[]{:S(2)}, u32[]{:S(2)}) collective-permute-start(bf16[4,32,256]{2,1,0:T(8,128)(2,1)S(1)} %slice.46), channel_id=1, source_target_pairs={{0,4},{4,8},{8,12},{1,5},{5,9},{9,13},{2,6},{6,10},{10,14},{3,7},{... | collective-permute-start | bytes 196616 | tf_op jit(solution)/shard_map/ppermute | solution.py:24
Sparse Core Ops, SparseCore 0:
  91.0 13.4 reduce-scatter.2
  130.3 79.2 reduce-scatter.4

commit v2 on v1

--- a/solution.py
+++ b/solution.py
@@ -26,12 +26,13 @@
 
 def dx_kernel(r_ref, t_ref, o_ref, *, lag_tiles, rows):
     width = o_ref.shape[2]
+    width_t = t_ref.shape[2]
     for c in range(rows // chunk_rows):
         base = c * chunk_rows
         acc = jnp.zeros((chunk_rows, width), jnp.float32)
         for q in range(lag_tiles):
             x = r_ref[0, base + q : base + q + chunk_rows, :].astype(jnp.bfloat16)
-            acc = acc + jnp.dot(x, t_ref[0, q], preferred_element_type=jnp.float32)
+            acc = acc + jnp.dot(x, t_ref[0, q * width_t : (q + 1) * width_t, :], preferred_element_type=jnp.float32)
         o_ref[0, base : base + chunk_rows, :] = acc
 
 
@@ -99,21 +100,17 @@
 
     kern = impulse.reshape(nb, lag_count, width, width)
     kpad = jnp.pad(kern, ((0, 0), (tr - 1, tr), (0, 0), (0, 0)))
-    rows_of = []
-    for s in range(tr):
-        cols_of = []
-        for u in range(tr):
-            start = s - u + tr - 1
-            cols_of.append(lax.slice_in_dim(kpad, start, start + tr * shift + 1, tr, 1))
-        rows_of.append(jnp.stack(cols_of, axis=3))
-    toeplitz = jnp.stack(rows_of, axis=2).reshape(nb, lag_tiles, wide, wide)
+    stripes = tr * lag_tiles
+    toeplitz = jnp.concatenate(
+        [lax.slice_in_dim(kpad, tr - 1 - u, tr - 1 - u + stripes, 1, 1) for u in range(tr)], axis=3
+    ).reshape(nb, stripes * width, wide)
 
     partial_dx = pl.pallas_call(
         functools.partial(dx_kernel, lag_tiles=lag_tiles, rows=rows4),
         grid=(nb,),
         in_specs=[
             pl.BlockSpec((1, rows4 + shift, wide), lambda b: (b, 0, 0)),
-            pl.BlockSpec((1, lag_tiles, wide, wide), lambda b: (b, 0, 0, 0)),
+            pl.BlockSpec((1, tr * lag_tiles * width, wide), lambda b: (b, 0, 0)),
         ],
         out_specs=pl.BlockSpec((1, rows4, wide), lambda b: (b, 0, 0)),
         out_shape=jax.ShapeDtypeStruct((nb, rows4, wide), jnp.float32),

time: 258 us -> 215 us (0.83)
  local copies, waits for them, and re-layouts: 73.3 us -> 36.2 us
  other arithmetic: 28.9 us -> 24.5 us
    reshape x1 -> x0, local copies, waits for them, and re-layouts: 25.6 us -> none  [local(): toeplitz = jnp.stack(rows_of, axis=2).reshape(nb, lag_tiles, wide, wide)]
    another operation x2 -> x0, local copies, waits for them, and re-layouts: 20.8 us -> none  [the longest x1 16.5 us: local(): toeplitz = jnp.stack(rows_of, axis=2).reshape(nb, lag_tiles, wide, wide)]
    another operation x2 -> x0, other arithmetic: 12.7 us -> none  [local(): toeplitz = jnp.stack(rows_of, axis=2).reshape(nb, lag_tiles, wide, wide)]
    slice x0 -> x1, local copies, waits for them, and re-layouts: none -> 9.33 us  [local(): lax.slice_in_dim(kpad, tr - 1 - u, tr - 1 - u + stripes, 1, 1)]
    concatenate x0 -> x1, other arithmetic: none -> 8.23 us  [local(): jnp.concatenate([lax.slice_in_dim(kpad, tr - 1 - u, tr - 1 - u + stripes,...]
  transfers between devices with their start and end apart: 4 -> 4, of which waited for: 2 -> 2; matrix products, arithmetic and copies ran while one was open for 35% -> 23% of each run, Pallas kernels for 3% -> 4%
where the time goes in v2:
time: 215 us
  waiting for transfers between devices  78.5 us (37%)
  local copies, waits for them, and re-layouts  36.2 us (17%)
  blocking collectives  33.2 us (15%)
  other arithmetic  24.5 us (11%)
  Pallas kernels  17.6 us (8%)
  between operations  15.5 us (7%)
  starting transfers between devices  7.13 us (3%)
    reduce_scatter x1, waiting for transfers between devices, local(): lax.psum_scatter(grad_flat, 'tm', scatter_dimension=2, tiled=True)  76.8 us
    psum x1, blocking collectives, local(): total_squares = lax.psum(own_squares, ('tm', 'bundle', 'sub'))  33.2 us
    slice x1, local copies, waits for them, and re-layouts, local(): lax.slice_in_dim(kpad, tr - 1 - u, tr - 1 - u + stripes, 1, 1)  9.33 us
    pallas_call x1, Pallas kernels, local(): pl.pallas_call(functools.partial(raw_kernel, shift=shift, rows=rows4, wid...  8.82 us
    pallas_call x1, Pallas kernels, local(): pl.pallas_call(functools.partial(dx_kernel, lag_tiles=lag_tiles, rows=row...  8.8 us
    select_n x1, other arithmetic, local(): jnp.where(live4[None, :, :, None], inp4, jnp.zeros((), jnp.bfloat16))  8.24 us
    concatenate x1, other arithmetic, local(): jnp.concatenate([lax.slice_in_dim(kpad, tr - 1 - u, tr - 1 - u + stripes,...  8.23 us
    reshape x1, local copies, waits for them, and re-layouts, local(): grad_flat = raw.reshape(nb, lag_count, width * width)  7.89 us
  transfers between devices with their start and end apart: 4, of which 2 were waited for; matrix products, arithmetic and copies ran while one was open for 23% of the time, Pallas kernels for 4%

profile of v2, /device:TPU:0, one launch (start us, length us, event | category | flops | bytes accessed | tf_op | source)
XLA Modules:
  0.0 214.7 jit_solution(8458114399347834092)
XLA Ops:
  7.2 3.3 %reshape.95 = bf16[512,4,4,64]{3,2,1,0:T(4,128)(2,1)S(1)} reshape(bf16[2048,256]{1,0:T(8,128)(2,1)} %param.5) | data formatting | bytes 2097152 | tf_op jit(solution)/shard_map/reshape | solution.py:81
  10.5 2.0 fusion.2
  12.5 0.5 copy.13
  13.1 1.3 collective-permute-start
  14.4 6.9 %reshape.97 = bf16[4,64,64,64]{3,2,1,0:T(8,128)(2,1)} reshape(bf16[4,64,4096]{2,1,0:T(8,128)(2,1)} %param.7) | data formatting | bytes 4194304 | tf_op jit(solution)/shard_map/reshape | solution.py:101
  21.3 9.3 %pad_slice_fusion.3 = (bf16[4,68,64,64]{3,2,1,0:T(8,128)(2,1)S(1)}, bf16[4,68,64,64]{3,2,1,0:T(8,128)(2,1)S(1)}, bf16[4,68,64,64]{3,2,1,0:T(8,128)(2,1)S(1)}, bf16[4,68,64,64]{3,2,1,0:T(8,128)(2,1)S(1)}) fusion(bf16[4,64,64,64]{3,2,1,0:T(8,128)(2,1)} %reshape.97), kind=kLoop, calls=%fused_computation.4 | loop fusion | bytes 11010048 | tf_op jit(solution)/shard_map/slice | solution.py:105
  30.6 8.2 %pad_maximum_fusion = bf16[4,68,64,256]{3,2,1,0:T(8,128)(2,1)} fusion(bf16[4,68,64,64]{3,2,1,0:T(8,128)(2,1)S(1)} %get-tuple-element.5, bf16[4,68,64,64]{3,2,1,0:T(8,128)(2,1)S(1)} %get-tuple-element.4, bf16[4,68,64,64]{3,2,1,0:T(8,128)(2,1)S(1)} %get-tuple-element.3, bf16[4,68,64,64]{3,2,1,0:T(8,128)(2,1)S(1)} %get-tuple-element.2), kind=kLoop, calls=%fused_computation | loop fusion | flops 35651584 | bytes 17825792 | tf_op jit(solution)/shard_map/concatenate | solution.py:104
  38.8 1.8 fusion.8.r_ref
  40.6 8.8 %shard_map.68 = f32[4,512,256]{2,1,0:T(8,128)} custom-call(f32[4,528,256]{2,1,0:T(8,128)} %fusion.8.r_ref, bf16[4,4352,256]{2,1,0:T(8,128)(2,1)} %bitcast.23), custom_call_target="tpu_custom_call" | custom-call | tf_op jit(solution)/shard_map/pallas_call | solution.py:108
  50.1 0.9 reshape.102
  51.2 8.2 %select_bitcast_fusion = bf16[4,512,4,64]{3,0,2,1:T(4,128)(2,1)} fusion(bf16[512,4,4,64]{3,2,1,0:T(4,128)(2,1)S(1)} %reshape.102, pred[512,4]{1,0:T(8,128)(4,1)S(1)} %add_compare_fusion), kind=kLoop, calls=%fused_computation.7 | loop fusion | flops 524288 | bytes 2099200 | tf_op jit(solution)/shard_map/jit(_where)/select_n | solution.py:92
  59.4 3.0 %copy.16 = bf16[4,512,4,64]{1,3,2,0:T(8,128)(2,1)S(1)} copy(bf16[4,512,4,64]{3,0,2,1:T(4,128)(2,1)} %select_bitcast_fusion) | data formatting | bytes 2097152 | tf_op jit(solution)/shard_map/jit(_where)/select_n | solution.py:92
  62.9 5.8 %collective-permute-start.1 = (bf16[4,32,256]{2,1,0:T(8,128)(2,1)S(1)}, bf16[4,32,256]{2,1,0:T(8,128)(2,1)S(1)}, u32[]{:S(2)}, u32[]{:S(2)}) collective-permute-start(bf16[4,32,256]{2,1,0:T(8,128)(2,1)S(1)} %slice.25), channel_id=1, source_target_pairs={{0,4},{4,8},{8,12},{1,5},{5,9},{9,13},{2,6},{6,10},{10,14},{3,7},{... | collective-permute-start | bytes 196616 | tf_op jit(solution)/shard_map/ppermute | solution.py:24
  68.7 1.7 collective-permute-done.1
  70.4 1.6 fusion.6.m_ref
  72.0 8.8 %shard_map.69 = f32[4,64,64,64]{3,2,1,0:T(8,128)} custom-call(bf16[4,256,512]{2,1,0:T(8,128)(2,1)} %bitcast.25, f32[4,528,256]{2,1,0:T(8,128)} %fusion.6.m_ref), custom_call_target="tpu_custom_call" | custom-call | tf_op jit(solution)/shard_map/pallas_call | solution.py:120
  80.8 7.9 %reshape.104 = f32[4,64,4096]{2,1,0:T(8,128)} reshape(f32[4,64,64,64]{3,2,1,0:T(8,128)} %shard_map.69) | data formatting | bytes 8388608 | tf_op jit(solution)/shard_map/reshape | solution.py:147
  88.8 1.4 copy.14
  90.3 1.0 copy.15
  91.3 76.8 %reduce-scatter.5.cloned.1.call-done = f32[4,64,1024]{2,1,0:T(8,128)} async-done(((f32[4,64,4096]{2,1,0:T(8,128)}), f32[4,64,1024]{2,1,0:T(8,128)}) %reduce-scatter.5.cloned.1.call-update) | async-done | bytes 1048592 | tf_op jit(solution)/shard_map/reduce_scatter | solution.py:148
  168.1 2.1 multiply_reduce_fusion
  170.2 1.5 reshape.100
  171.6 33.2 %psum.7 = f32[]{:T(128)} all-reduce(f32[]{:T(128)} %multiply_reduce_fusion), channel_id=1, replica_groups=mesh['case'=2,'tm'=4,'bundle'=2,'sub'=2] {'tm','bundle','sub'}, use_global_device_ids=true, to_apply=%region_3.4 | all-reduce | flops 1 | bytes 8 | tf_op jit(solution)/shard_map/psum | solution.py:150
  205.5 2.3 %broadcast_multiply_fusion = f32[4,64,1024]{2,1,0:T(8,128)} fusion(f32[4,64,1024]{2,1,0:T(8,128)} %reduce-scatter.5.cloned.1.call-done, f32[]{:T(128)S(6)} %div.3), kind=kLoop, calls=%fused_computation.20 | loop fusion | flops 262144 | bytes 2097156 | tf_op jit(solution)/shard_map/mul | solution.py:153
  (18 shorter events, 0.9 us)
Async XLA Ops:
  7.2 81.6 %reduce-scatter.3.cloned.1.call-start = ((), (), s32[]{:S(2)}) async-start(), calls=%async_computation.2 | async-start | bytes 3145728 | tf_op jit(solution)/shard_map/reduce_scatter | solution.py:132
  12.5 8.8 %copy-start = (bf16[4,64,512,4]{2,1,3,0:T(8,128)(2,1)}, bf16[4,64,512,4]{2,1,3,0:T(8,128)(2,1)S(1)}, u32[]{:S(2)}) copy-start(bf16[4,64,512,4]{2,1,3,0:T(8,128)(2,1)S(1)} %fusion.2) | copy-start | bytes 3145732
  13.1 25.8 %collective-permute-start = (bf16[4,32,256]{2,1,0:T(8,128)(2,1)S(1)}, bf16[4,32,256]{2,1,0:T(8,128)(2,1)S(1)}, u32[]{:S(2)}, u32[]{:S(2)}) collective-permute-start(bf16[4,32,256]{2,1,0:T(8,128)(2,1)S(1)} %slice.24), channel_id=1, source_target_pairs={{4,0},{8,4},{12,8},{5,1},{9,5},{13,9},{6,2},{10,6},{14,10},{7,3},{... | collective-permute-start | bytes 196616 | tf_op jit(solution)/shard_map/ppermute | solution.py:24
  40.6 9.5 %copy-start.1 = (bf16[2048,256]{1,0:T(8,128)(2,1)S(1)}, bf16[2048,256]{1,0:T(8,128)(2,1)}, u32[]{:S(2)}) copy-start(bf16[2048,256]{1,0:T(8,128)(2,1)} %param.6) | copy-start | bytes 3145732
  49.4 118.6 %reduce-scatter.5.cloned.1.call-start = ((), (), s32[]{:S(2)}) async-start(), calls=%async_computation.3 | async-start | bytes 5242880 | tf_op jit(solution)/shard_map/reduce_scatter | solution.py:148
  62.9 7.5 %collective-permute-start.1 = (bf16[4,32,256]{2,1,0:T(8,128)(2,1)S(1)}, bf16[4,32,256]{2,1,0:T(8,128)(2,1)S(1)}, u32[]{:S(2)}, u32[]{:S(2)}) collective-permute-start(bf16[4,32,256]{2,1,0:T(8,128)(2,1)S(1)} %slice.25), channel_id=1, source_target_pairs={{0,4},{4,8},{8,12},{1,5},{5,9},{9,13},{2,6},{6,10},{10,14},{3,7},{... | collective-permute-start | bytes 196616 | tf_op jit(solution)/shard_map/ppermute | solution.py:24
Sparse Core Ops, SparseCore 0:
  49.5 13.4 reduce-scatter.2
  88.8 79.1 reduce-scatter.4

commit v3 on v2

--- a/solution.py
+++ b/solution.py
@@ -147,7 +147,9 @@
     grad_flat = raw.reshape(nb, lag_count, width * width)
     own_grad = lax.psum_scatter(grad_flat, "tm", scatter_dimension=2, tiled=True)
     own_squares = jnp.sum(own_grad * own_grad)
-    total_squares = lax.psum(own_squares, ("tm", "bundle", "sub"))
+    total_squares = own_squares
+    for axis in ("sub", "bundle", "tm"):
+        total_squares = lax.psum(total_squares, axis)
     norm_limit = norm_ratio * math.sqrt(NB * L * CB * CB)
     factor = norm_limit / jnp.sqrt(total_squares + 1e-06)
     return (voltage_grad, own_grad * factor)

time: 215 us -> 202 us (0.940)
  blocking collectives: 33.2 us -> 20.2 us
    psum x1 -> x3, blocking collectives: 33.2 us -> 20.2 us  [local(): total_squares = lax.psum(total_squares, axis)]
  transfers between devices with their start and end apart: 4 -> 4, of which waited for: 2 -> 2; matrix products, arithmetic and copies ran while one was open for 23% -> 24% of each run, Pallas kernels for 4% -> 4%
where the time goes in v3:
time: 202 us
  waiting for transfers between devices  79.6 us (39%)
  local copies, waits for them, and re-layouts  36.2 us (18%)
  other arithmetic  23.3 us (12%)
  blocking collectives  20.2 us (10%)
  Pallas kernels  17.6 us (9%)
  between operations  15.6 us (8%)
  starting transfers between devices  7.13 us (4%)
    reduce_scatter x1, waiting for transfers between devices, local(): lax.psum_scatter(grad_flat, 'tm', scatter_dimension=2, tiled=True)  77.9 us
    psum x3, blocking collectives, local(): total_squares = lax.psum(total_squares, axis)  20.2 us
    slice x1, local copies, waits for them, and re-layouts, local(): lax.slice_in_dim(kpad, tr - 1 - u, tr - 1 - u + stripes, 1, 1)  9.33 us
    pallas_call x1, Pallas kernels, local(): pl.pallas_call(functools.partial(raw_kernel, shift=shift, rows=rows4, wid...  8.82 us
    pallas_call x1, Pallas kernels, local(): pl.pallas_call(functools.partial(dx_kernel, lag_tiles=lag_tiles, rows=row...  8.8 us
    select_n x1, other arithmetic, local(): jnp.where(live4[None, :, :, None], inp4, jnp.zeros((), jnp.bfloat16))  8.24 us
    concatenate x1, other arithmetic, local(): jnp.concatenate([lax.slice_in_dim(kpad, tr - 1 - u, tr - 1 - u + stripes,...  8.23 us
    reshape x1, local copies, waits for them, and re-layouts, local(): grad_flat = raw.reshape(nb, lag_count, width * width)  7.89 us
  transfers between devices with their start and end apart: 4, of which 2 were waited for; matrix products, arithmetic and copies ran while one was open for 24% of the time, Pallas kernels for 4%

profile of v3, /device:TPU:0, one launch (start us, length us, event | category | flops | bytes accessed | tf_op | source)
XLA Modules:
  0.0 201.6 jit_solution(4865635973872560519)
XLA Ops:
  7.2 3.3 %reshape.95 = bf16[512,4,4,64]{3,2,1,0:T(4,128)(2,1)S(1)} reshape(bf16[2048,256]{1,0:T(8,128)(2,1)} %param.5) | data formatting | bytes 2097152 | tf_op jit(solution)/shard_map/reshape | solution.py:81
  10.5 2.0 fusion.2
  13.1 1.3 collective-permute-start
  14.4 6.9 %reshape.97 = bf16[4,64,64,64]{3,2,1,0:T(8,128)(2,1)} reshape(bf16[4,64,4096]{2,1,0:T(8,128)(2,1)} %param.7) | data formatting | bytes 4194304 | tf_op jit(solution)/shard_map/reshape | solution.py:101
  21.3 9.3 %pad_slice_fusion.3 = (bf16[4,68,64,64]{3,2,1,0:T(8,128)(2,1)S(1)}, bf16[4,68,64,64]{3,2,1,0:T(8,128)(2,1)S(1)}, bf16[4,68,64,64]{3,2,1,0:T(8,128)(2,1)S(1)}, bf16[4,68,64,64]{3,2,1,0:T(8,128)(2,1)S(1)}) fusion(bf16[4,64,64,64]{3,2,1,0:T(8,128)(2,1)} %reshape.97), kind=kLoop, calls=%fused_computation.4 | loop fusion | bytes 11010048 | tf_op jit(solution)/shard_map/slice | solution.py:105
  30.6 8.2 %pad_maximum_fusion = bf16[4,68,64,256]{3,2,1,0:T(8,128)(2,1)} fusion(bf16[4,68,64,64]{3,2,1,0:T(8,128)(2,1)S(1)} %get-tuple-element.5, bf16[4,68,64,64]{3,2,1,0:T(8,128)(2,1)S(1)} %get-tuple-element.4, bf16[4,68,64,64]{3,2,1,0:T(8,128)(2,1)S(1)} %get-tuple-element.3, bf16[4,68,64,64]{3,2,1,0:T(8,128)(2,1)S(1)} %get-tuple-element.2), kind=kLoop, calls=%fused_computation | loop fusion | flops 35651584 | bytes 17825792 | tf_op jit(solution)/shard_map/concatenate | solution.py:104
  38.8 1.8 fusion.8.r_ref
  40.6 8.8 %shard_map.68 = f32[4,512,256]{2,1,0:T(8,128)} custom-call(f32[4,528,256]{2,1,0:T(8,128)} %fusion.8.r_ref, bf16[4,4352,256]{2,1,0:T(8,128)(2,1)} %bitcast.23), custom_call_target="tpu_custom_call" | custom-call | tf_op jit(solution)/shard_map/pallas_call | solution.py:108
  51.2 8.2 %select_bitcast_fusion = bf16[4,512,4,64]{3,0,2,1:T(4,128)(2,1)} fusion(bf16[512,4,4,64]{3,2,1,0:T(4,128)(2,1)S(1)} %reshape.102, pred[512,4]{1,0:T(8,128)(4,1)S(1)} %add_compare_fusion), kind=kLoop, calls=%fused_computation.7 | loop fusion | flops 524288 | bytes 2099200 | tf_op jit(solution)/shard_map/jit(_where)/select_n | solution.py:92
  59.4 3.0 %copy.16 = bf16[4,512,4,64]{1,3,2,0:T(8,128)(2,1)S(1)} copy(bf16[4,512,4,64]{3,0,2,1:T(4,128)(2,1)} %select_bitcast_fusion) | data formatting | bytes 2097152 | tf_op jit(solution)/shard_map/jit(_where)/select_n | solution.py:92
  62.9 5.8 %collective-permute-start.1 = (bf16[4,32,256]{2,1,0:T(8,128)(2,1)S(1)}, bf16[4,32,256]{2,1,0:T(8,128)(2,1)S(1)}, u32[]{:S(2)}, u32[]{:S(2)}) collective-permute-start(bf16[4,32,256]{2,1,0:T(8,128)(2,1)S(1)} %slice.25), channel_id=1, source_target_pairs={{0,4},{4,8},{8,12},{1,5},{5,9},{9,13},{2,6},{6,10},{10,14},{3,7},{... | collective-permute-start | bytes 196616 | tf_op jit(solution)/shard_map/ppermute | solution.py:24
  68.7 1.7 collective-permute-done.1
  70.4 1.6 fusion.6.m_ref
  72.0 8.8 %shard_map.69 = f32[4,64,64,64]{3,2,1,0:T(8,128)} custom-call(bf16[4,256,512]{2,1,0:T(8,128)(2,1)} %bitcast.25, f32[4,528,256]{2,1,0:T(8,128)} %fusion.6.m_ref), custom_call_target="tpu_custom_call" | custom-call | tf_op jit(solution)/shard_map/pallas_call | solution.py:120
  80.8 7.9 %reshape.104 = f32[4,64,4096]{2,1,0:T(8,128)} reshape(f32[4,64,64,64]{3,2,1,0:T(8,128)} %shard_map.69) | data formatting | bytes 8388608 | tf_op jit(solution)/shard_map/reshape | solution.py:147
  88.8 1.4 copy.14
  90.2 77.9 %reduce-scatter.5.cloned.1.call-done = f32[4,64,1024]{2,1,0:T(8,128)} async-done(((f32[4,64,4096]{2,1,0:T(8,128)}), f32[4,64,1024]{2,1,0:T(8,128)}) %reduce-scatter.5.cloned.1.call-update) | async-done | bytes 1048592 | tf_op jit(solution)/shard_map/reduce_scatter | solution.py:148
  168.1 2.2 %multiply_reduce_fusion = f32[]{:T(128)} fusion(f32[4,64,1024]{2,1,0:T(8,128)} %reduce-scatter.5.cloned.1.call-done), kind=kLoop, calls=%fused_computation.17 | loop fusion | flops 524287 | bytes 1048580 | tf_op jit(solution)/shard_map/reduce_sum | solution.py:149
  170.4 3.1 %psum.21 = f32[]{:T(128)} all-reduce(f32[]{:T(128)} %multiply_reduce_fusion), channel_id=1, replica_groups=mesh['case'=2,'tm'=4,'bundle'=2,'sub'=2] {'sub'}, use_global_device_ids=true, to_apply=%region_3.4 | all-reduce | flops 1 | bytes 8 | tf_op jit(solution)/shard_map/psum | solution.py:152
  173.5 1.0 copy.15
  174.4 5.6 %psum.22 = f32[]{:T(128)} all-reduce(f32[]{:T(128)} %psum.21), channel_id=1, replica_groups=mesh['case'=2,'tm'=4,'bundle'=2,'sub'=2] {'bundle'}, use_global_device_ids=true, to_apply=%region_4.5 | all-reduce | flops 1 | bytes 8 | tf_op jit(solution)/shard_map/psum | solution.py:152
  180.0 1.5 reshape.100
  181.5 11.6 %psum.23 = f32[]{:T(128)} all-reduce(f32[]{:T(128)} %psum.22), channel_id=1, replica_groups=mesh['case'=2,'tm'=4,'bundle'=2,'sub'=2] {'tm'}, use_global_device_ids=true, to_apply=%region_5.6 | all-reduce | flops 1 | bytes 8 | tf_op jit(solution)/shard_map/psum | solution.py:152
  193.8 1.0 broadcast_multiply_fusion
  (22 shorter events, 2.3 us)
Async XLA Ops:
  7.2 81.6 %reduce-scatter.3.cloned.1.call-start = ((), (), s32[]{:S(2)}) async-start(), calls=%async_computation.2 | async-start | bytes 3145728 | tf_op jit(solution)/shard_map/reduce_scatter | solution.py:132
  12.5 8.8 %copy-start = (bf16[4,64,512,4]{2,1,3,0:T(8,128)(2,1)}, bf16[4,64,512,4]{2,1,3,0:T(8,128)(2,1)S(1)}, u32[]{:S(2)}) copy-start(bf16[4,64,512,4]{2,1,3,0:T(8,128)(2,1)S(1)} %fusion.2) | copy-start | bytes 3145732
  13.1 25.8 %collective-permute-start = (bf16[4,32,256]{2,1,0:T(8,128)(2,1)S(1)}, bf16[4,32,256]{2,1,0:T(8,128)(2,1)S(1)}, u32[]{:S(2)}, u32[]{:S(2)}) collective-permute-start(bf16[4,32,256]{2,1,0:T(8,128)(2,1)S(1)} %slice.24), channel_id=1, source_target_pairs={{4,0},{8,4},{12,8},{5,1},{9,5},{13,9},{6,2},{10,6},{14,10},{7,3},{... | collective-permute-start | bytes 196616 | tf_op jit(solution)/shard_map/ppermute | solution.py:24
  40.6 9.5 %copy-start.2 = (bf16[2048,256]{1,0:T(8,128)(2,1)S(1)}, bf16[2048,256]{1,0:T(8,128)(2,1)}, u32[]{:S(2)}) copy-start(bf16[2048,256]{1,0:T(8,128)(2,1)} %param.6) | copy-start | bytes 3145732
  49.4 118.6 %reduce-scatter.5.cloned.1.call-start = ((), (), s32[]{:S(2)}) async-start(), calls=%async_computation.3 | async-start | bytes 5242880 | tf_op jit(solution)/shard_map/reduce_scatter | solution.py:148
  62.9 7.5 %collective-permute-start.1 = (bf16[4,32,256]{2,1,0:T(8,128)(2,1)S(1)}, bf16[4,32,256]{2,1,0:T(8,128)(2,1)S(1)}, u32[]{:S(2)}, u32[]{:S(2)}) collective-permute-start(bf16[4,32,256]{2,1,0:T(8,128)(2,1)S(1)} %slice.25), channel_id=1, source_target_pairs={{0,4},{4,8},{8,12},{1,5},{5,9},{9,13},{2,6},{6,10},{10,14},{3,7},{... | collective-permute-start | bytes 196616 | tf_op jit(solution)/shard_map/ppermute | solution.py:24
  168.1 25.7 %copy-start.1 = (f32[4,64,1024]{2,1,0:T(8,128)S(1)}, f32[4,64,1024]{2,1,0:T(8,128)}, u32[]{:S(2)}) copy-start(f32[4,64,1024]{2,1,0:T(8,128)} %reduce-scatter.5.cloned.1.call-done) | copy-start | bytes 3145732
Sparse Core Ops, SparseCore 0:
  49.5 13.4 reduce-scatter.2
  88.8 79.1 reduce-scatter.4

commit v4 on v3

--- a/solution.py
+++ b/solution.py
@@ -5,6 +5,7 @@
 import jax.numpy as jnp
 from jax import lax
 from jax.experimental import pallas as pl
+from jax.experimental.pallas import tpu as pltpu
 from jax.sharding import PartitionSpec as P
 
 CB = 64
@@ -24,6 +25,10 @@
     return lax.ppermute(block, axis, route)
 
 
+def lags_span(all_lags, band):
+    return band * (all_lags // band + 1) + 1
+
+
 def dx_kernel(r_ref, t_ref, o_ref, *, lag_tiles, rows):
     width = o_ref.shape[2]
     width_t = t_ref.shape[2]
@@ -36,29 +41,20 @@
         o_ref[0, base : base + chunk_rows, :] = acc
 
 
-def raw_kernel(rt_ref, m_ref, o_ref, *, shift, rows, width):
+def raw_kernel(rt_ref, m_ref, o_ref, acc_ref, *, lag_steps, rows, chunk, pad, lags):
+    band = 16
+    acc_ref[...] = jnp.zeros(acc_ref.shape, jnp.float32)
     rt = rt_ref[0]
-
-    def corr(q):
-        m = m_ref[0, shift - q : shift - q + rows, :].astype(jnp.bfloat16)
-        return jnp.dot(rt, m, preferred_element_type=jnp.float32)
-
-    g_prev = corr(0)
-    for a in range(shift):
-        g_next = corr(a + 1)
-        for d in range(tile_rows):
-            acc = None
-            for s in range(tile_rows):
-                u = s - d
-                if 0 <= u < tile_rows:
-                    blk = g_prev[s * width : (s + 1) * width, u * width : (u + 1) * width]
-                    acc = blk if acc is None else acc + blk
-                u = s - d + tile_rows
-                if 0 <= u < tile_rows:
-                    blk = g_next[s * width : (s + 1) * width, u * width : (u + 1) * width]
-                    acc = blk if acc is None else acc + blk
-            o_ref[0, tile_rows * a + d] = acc
-        g_prev = g_next
+    top = lag_steps - 1
+    for q in range(lag_steps):
+        m = m_ref[0, top - q : top - q + rows, :].astype(jnp.bfloat16)
+        g = jnp.dot(rt, m, preferred_element_type=jnp.float32)
+        for v in range(band // 2):
+            first = (band * q - 2 * v + pad) * chunk
+            acc_ref[first : first + band * chunk, :] += g[:, v * 2 * CB : (v + 1) * 2 * CB]
+    lo = acc_ref[pad * chunk : (pad + lags) * chunk, :]
+    hi = acc_ref[(pad + 1) * chunk : (pad + 1 + lags) * chunk, :]
+    o_ref[0] = lo[:, :CB] + hi[:, CB:]
 
 
 def local(cotangent, inputs, impulse, terminal, fault_step):
@@ -83,7 +79,6 @@
         "ksbi,bir->bksr", cot4, onehot, preferred_element_type=jnp.float32
     ).astype(jnp.bfloat16)
     r4 = reord4.reshape(nb, rows4, wide)
-    r4t = jnp.transpose(reord4, (0, 2, 3, 1)).reshape(nb, wide, rows4)
 
     seg_start = lax.axis_index("tm") * seg_rows
     steps4 = seg_start + tr * jnp.arange(rows4, dtype=jnp.int32)[:, None] + jnp.arange(tr, dtype=jnp.int32)[None, :]
@@ -94,10 +89,6 @@
     ahead = passed_along(r4[:, :halo], "tm", -1)
     r4ext = jnp.concatenate([r4, ahead], axis=1).astype(jnp.float32)
     r4w = lax.dynamic_slice_in_dim(r4ext, sub * shift, rows4 + shift, 1)
-    behind = passed_along(m4[:, rows4 - halo :], "tm", 1)
-    m4ext = jnp.concatenate([behind, m4], axis=1).astype(jnp.float32)
-    m4w = lax.dynamic_slice_in_dim(m4ext, (n_sub - 1 - sub) * shift, rows4 + shift, 1)
-
     kern = impulse.reshape(nb, lag_count, width, width)
     kpad = jnp.pad(kern, ((0, 0), (tr - 1, tr), (0, 0), (0, 0)))
     stripes = tr * lag_tiles
@@ -117,17 +108,36 @@
         interpret=_INTERPRET,
     )(r4w, toeplitz)
 
-    raw = pl.pallas_call(
-        functools.partial(raw_kernel, shift=shift, rows=rows4, width=width),
-        grid=(nb,),
+    n_tm = lax.axis_size("tm")
+    half = nb // n_sub
+    chunk = width // n_tm
+    band = 16
+    rows16 = seg_rows * n_tm // band
+    lag_steps = all_lags // band + 1
+    pad = band
+    mine = lax.dynamic_slice_in_dim(m4.reshape(nb, seg_rows, width), sub * half, half, 0)
+    m_all = lax.all_gather(mine, "tm", axis=1, tiled=True)
+    m16 = m_all.reshape(half, rows16, band * width)
+    m16 = jnp.pad(m16, ((0, 0), (lag_steps - 1, 0), (0, 0))).astype(jnp.float32)
+    reord_mine = lax.dynamic_slice_in_dim(r4.reshape(nb, seg_rows, width), sub * half, half, 0)
+    r_split = reord_mine.reshape(half, seg_rows, n_tm, chunk)
+    r_all = lax.all_to_all(r_split, "tm", 2, 1, tiled=True)
+    r16t = jnp.transpose(r_all.reshape(half, rows16, band, chunk), (0, 2, 3, 1)).reshape(half, band * chunk, rows16)
+    acc_rows = (pad + lags_span(all_lags, band) + pad) * chunk
+    raw_half = pl.pallas_call(
+        functools.partial(raw_kernel, lag_steps=lag_steps, rows=rows16, chunk=chunk, pad=pad, lags=all_lags),
+        grid=(half,),
         in_specs=[
-            pl.BlockSpec((1, wide, rows4), lambda b: (b, 0, 0)),
-            pl.BlockSpec((1, rows4 + shift, wide), lambda b: (b, 0, 0)),
+            pl.BlockSpec((1, band * chunk, rows16), lambda b: (b, 0, 0)),
+            pl.BlockSpec((1, rows16 + lag_steps - 1, band * width), lambda b: (b, 0, 0)),
         ],
-        out_specs=pl.BlockSpec((1, lag_count, width, width), lambda b: (b, 0, 0, 0)),
-        out_shape=jax.ShapeDtypeStruct((nb, lag_count, width, width), jnp.float32),
+        out_specs=pl.BlockSpec((1, all_lags * chunk, width), lambda b: (b, 0, 0)),
+        out_shape=jax.ShapeDtypeStruct((half, all_lags * chunk, width), jnp.float32),
+        scratch_shapes=[pltpu.VMEM((acc_rows, 2 * width), jnp.float32)],
         interpret=_INTERPRET,
-    )(r4t, m4w)
+    )(r16t, m16)
+    raw_half = raw_half.reshape(half, all_lags, chunk * width)
+    own_raw = lax.all_to_all(raw_half, "sub", 1, 0, tiled=True)
 
     summed_dx = lax.psum_scatter(partial_dx, "sub", scatter_dimension=1, tiled=True)
     share4 = summed_dx.shape[1]
@@ -144,8 +154,7 @@
     ).astype(jnp.bfloat16)
     voltage_grad = jnp.transpose(dx, (1, 2, 0, 3)).reshape(share4 * tr, nb * width)
 
-    grad_flat = raw.reshape(nb, lag_count, width * width)
-    own_grad = lax.psum_scatter(grad_flat, "tm", scatter_dimension=2, tiled=True)
+    own_grad = own_raw
     own_squares = jnp.sum(own_grad * own_grad)
     total_squares = own_squares
     for axis in ("sub", "bundle", "tm"):

time: 202 us -> 174 us (0.86)
  waiting for transfers between devices: 79.6 us -> 36.4 us
  local copies, waits for them, and re-layouts: 36.2 us -> 48.7 us
  blocking collectives: 20.2 us -> 22.8 us
    reduce_scatter x1 -> x0, waiting for transfers between devices: 77.9 us -> none  [local(): lax.psum_scatter(grad_flat, 'tm', scatter_dimension=2, tiled=True)]
    all_to_all x0 -> x1, waiting for transfers between devices: none -> 29.6 us  [local(): r_all = lax.all_to_all(r_split, 'tm', 2, 1, tiled=True)]
    all_to_all x0 -> x1, starting transfers between devices: none -> 7.31 us  [local(): r_all = lax.all_to_all(r_split, 'tm', 2, 1, tiled=True)]
    all_gather x0 -> x1, waiting for transfers between devices: none -> 6.76 us  [local(): m_all = lax.all_gather(mine, 'tm', axis=1, tiled=True)]
    ppermute x2 -> x1, starting transfers between devices: 7.05 us -> 1.29 us  [passed_along(): return lax.ppermute(block, axis, route)]
    reshape x2 -> x5, local copies, waits for them, and re-layouts: 8.41 us -> 13.4 us  [the longest x1 5.47 us: local(): m16 = m_all.reshape(half, rows16, band * width)]
    all_to_all x0 -> x1, blocking collectives: none -> 4.58 us  [local(): own_raw = lax.all_to_all(raw_half, 'sub', 1, 0, tiled=True)]
    transpose x0 -> x1, local copies, waits for them, and re-layouts: none -> 4.55 us  [local(): jnp.transpose(r_all.reshape(half, rows16, band, chunk), (0, 2, 3, 1))]
  transfers between devices with their start and end apart: 4 -> 4, of which waited for: 2 -> 2; matrix products, arithmetic and copies ran while one was open for 24% -> 32% of each run, Pallas kernels for 4% -> 10%
where the time goes in v4:
time: 174 us; the launch traced here: 173 us
  local copies, waits for them, and re-layouts  48.7 us (28%)
  waiting for transfers between devices  36.4 us (21%)
  blocking collectives  22.8 us (13%)
  other arithmetic  21.3 us (12%)
  between operations  17 us (10%)
  Pallas kernels  16.9 us (10%)
  starting transfers between devices  8.68 us (5%)
    all_to_all x1, waiting for transfers between devices, local(): r_all = lax.all_to_all(r_split, 'tm', 2, 1, tiled=True)  29.6 us
    psum x3, blocking collectives, local(): total_squares = lax.psum(total_squares, axis)  18.2 us
    slice x1, local copies, waits for them, and re-layouts, local(): lax.slice_in_dim(kpad, tr - 1 - u, tr - 1 - u + stripes, 1, 1)  9.44 us
    pallas_call x1, Pallas kernels, local(): pl.pallas_call(functools.partial(dx_kernel, lag_tiles=lag_tiles, rows=row...  8.76 us
    concatenate x1, other arithmetic, local(): jnp.concatenate([lax.slice_in_dim(kpad, tr - 1 - u, tr - 1 - u + stripes,...  8.23 us
    pallas_call x1, Pallas kernels, local(): pl.pallas_call(functools.partial(raw_kernel, lag_steps=lag_steps, rows=ro...  8.14 us
    all_to_all x1, starting transfers between devices, local(): r_all = lax.all_to_all(r_split, 'tm', 2, 1, tiled=True)  7.31 us
    select_n x1, other arithmetic, local(): jnp.where(live4[None, :, :, None], inp4, jnp.zeros((), jnp.bfloat16))  6.98 us
  transfers between devices with their start and end apart: 4, of which 2 were waited for; matrix products, arithmetic and copies ran while one was open for 32% of the time, Pallas kernels for 10%

profile of v4, /device:TPU:0, one launch (start us, length us, event | category | flops | bytes accessed | tf_op | source)
XLA Modules:
  0.0 173.0 jit_solution(14750670744342346133)
XLA Ops:
  8.7 3.3 %reshape.116 = bf16[512,4,4,64]{3,2,1,0:T(4,128)(2,1)S(1)} reshape(bf16[2048,256]{1,0:T(8,128)(2,1)} %param.6) | data formatting | bytes 2097152 | tf_op jit(solution)/shard_map/reshape | solution.py:86
  12.2 7.0 %broadcast_select_fusion = bf16[512,4,4,64]{3,2,1,0:T(4,128)(2,1)S(1)} fusion(bf16[512,4,4,64]{3,2,1,0:T(4,128)(2,1)S(1)} %reshape.116, pred[512,4]{1,0:T(8,128)(4,1)S(1)} %add_compare_fusion), kind=kLoop, calls=%fused_computation.8 | loop fusion | flops 524288 | bytes 2099200 | tf_op jit(solution)/shard_map/jit(_where)/select_n | solution.py:87
  25.5 6.9 %reshape.109 = bf16[4,64,64,64]{3,2,1,0:T(8,128)(2,1)} reshape(bf16[4,64,4096]{2,1,0:T(8,128)(2,1)} %param.7) | data formatting | bytes 4194304 | tf_op jit(solution)/shard_map/reshape | solution.py:92
  32.4 9.4 %pad_slice_fusion.3 = (bf16[4,68,64,64]{3,2,1,0:T(8,128)(2,1)S(1)}, bf16[4,68,64,64]{3,2,1,0:T(8,128)(2,1)S(1)}, bf16[4,68,64,64]{3,2,1,0:T(8,128)(2,1)S(1)}, bf16[4,68,64,64]{3,2,1,0:T(8,128)(2,1)S(1)}) fusion(bf16[4,64,64,64]{3,2,1,0:T(8,128)(2,1)} %reshape.109), kind=kLoop, calls=%fused_computation.4 | loop fusion | bytes 11010048 | tf_op jit(solution)/shard_map/slice | solution.py:96
  41.9 8.2 %pad_maximum_fusion = bf16[4,68,64,256]{3,2,1,0:T(8,128)(2,1)} fusion(bf16[4,68,64,64]{3,2,1,0:T(8,128)(2,1)S(1)} %get-tuple-element.5, bf16[4,68,64,64]{3,2,1,0:T(8,128)(2,1)S(1)} %get-tuple-element.4, bf16[4,68,64,64]{3,2,1,0:T(8,128)(2,1)S(1)} %get-tuple-element.3, bf16[4,68,64,64]{3,2,1,0:T(8,128)(2,1)S(1)} %get-tuple-element.2), kind=kLoop, calls=%fused_computation | loop fusion | flops 35651584 | bytes 17825792 | tf_op jit(solution)/shard_map/concatenate | solution.py:95
  50.1 1.7 fusion.6.r_ref
  51.8 8.8 %shard_map.68 = f32[4,512,256]{2,1,0:T(8,128)} custom-call(f32[4,528,256]{2,1,0:T(8,128)} %fusion.6.r_ref, bf16[4,4352,256]{2,1,0:T(8,128)(2,1)} %bitcast.33), custom_call_target="tpu_custom_call" | custom-call | tf_op jit(solution)/shard_map/pallas_call | solution.py:99
  60.6 1.4 copy.28
  63.2 7.3 %all-to-all-start = ((bf16[2,2048,4,16]{1,3,0,2:T(8,128)(2,1)}), bf16[2,2048,4,16]{1,3,0,2:T(8,128)(2,1)S(1)}, u32[]{:S(2)}, u32[]{:S(2)}) async-start(bf16[2,2048,4,16]{1,3,0,2:T(8,128)(2,1)} %copy.30), calls=%async_computation.1 | async-start | bytes 1048576 | tf_op jit(solution)/shard_map/all_to_all | solution.py:124
  70.6 29.6 %all-to-all-done = bf16[2,2048,4,16]{1,3,0,2:T(8,128)(2,1)S(1)} async-done(((bf16[2,2048,4,16]{1,3,0,2:T(8,128)(2,1)}), bf16[2,2048,4,16]{1,3,0,2:T(8,128)(2,1)S(1)}, u32[]{:S(2)}, u32[]{:S(2)}) %all-to-all-start) | async-done | bytes 524320 | tf_op jit(solution)/shard_map/all_to_all | solution.py:124
  100.6 4.3 %reshape.114 = bf16[2,512,16,16]{2,1,3,0:T(8,128)(2,1)} reshape(bf16[2,4,2048,1,16]{2,1,4,0,3:T(4,128)(2,1)S(1)} %copy.31) | data formatting | bytes 1048576 | tf_op jit(solution)/shard_map/reshape | solution.py:125
  104.9 4.6 %copy.32 = bf16[2,16,16,512]{3,2,1,0:T(8,128)(2,1)} copy(bf16[2,16,16,512]{1,3,2,0:T(8,128)(2,1)} %bitcast.34) | data formatting | bytes 1048576 | tf_op jit(solution)/shard_map/transpose | solution.py:125
  109.4 6.8 %all-gather.2.cloned.1.call-done = bf16[2,8192,64]{2,1,0:T(8,128)(2,1)} async-done(((bf16[2,2048,64]{2,1,0:T(8,128)(2,1)}), bf16[2,8192,64]{2,1,0:T(8,128)(2,1)}) %all-gather.2.cloned.1.call-update) | async-done | bytes 2097168 | tf_op jit(solution)/shard_map/all_gather | solution.py:119
  116.2 5.5 %reshape.117 = bf16[2,512,1024]{2,1,0:T(8,128)(2,1)S(1)} reshape(bf16[2,8192,64]{2,1,0:T(8,128)(2,1)} %all-gather.2.cloned.1.call-done) | data formatting | bytes 4194304 | tf_op jit(solution)/shard_map/reshape | solution.py:120
  121.7 2.4 %pad_convert_fusion.m_ref = f32[2,520,1024]{2,1,0:T(8,128)} fusion(bf16[2,512,1024]{2,1,0:T(8,128)(2,1)S(1)} %reshape.117), kind=kLoop, calls=%fused_computation.5 | loop fusion | flops 1064960 | bytes 6356992 | tf_op jit(solution)/shard_map/convert_element_type | solution.py:121
  124.1 8.1 %shard_map.69 = f32[2,2048,64]{2,1,0:T(8,128)} custom-call(bf16[2,256,512]{2,1,0:T(8,128)(2,1)} %bitcast.44, f32[2,520,1024]{2,1,0:T(8,128)} %pad_convert_fusion.m_ref), custom_call_target="tpu_custom_call" | custom-call | tf_op jit(solution)/shard_map/pallas_call | solution.py:127
  132.2 2.0 %reshape.118 = f32[2,128,1024]{2,1,0:T(8,128)S(1)} reshape(f32[2,2048,64]{2,1,0:T(8,128)} %shard_map.69) | data formatting | bytes 2097152 | tf_op jit(solution)/shard_map/reshape | solution.py:139
  135.1 4.6 %all_to_all.24 = f32[2,128,1024]{2,0,1:T(2,128)S(1)} all-to-all(f32[2,128,1024]{2,0,1:T(2,128)S(1)} %copy.34), channel_id=1, replica_groups=mesh['case'=2,'tm'=4,'bundle'=2,'sub'=2] {'sub'}, dimensions={1} | all-to-all | bytes 2097152 | tf_op jit(solution)/shard_map/all_to_all | solution.py:140
  139.7 1.7 multiply_reduce_fusion
  141.3 3.1 %psum.21 = f32[]{:T(128)} all-reduce(f32[]{:T(128)} %multiply_reduce_fusion), channel_id=1, replica_groups=mesh['case'=2,'tm'=4,'bundle'=2,'sub'=2] {'sub'}, use_global_device_ids=true, to_apply=%region_2.3 | all-reduce | flops 1 | bytes 8 | tf_op jit(solution)/shard_map/psum | solution.py:161
  144.4 5.5 %psum.22 = f32[]{:T(128)} all-reduce(f32[]{:T(128)} %psum.21), channel_id=1, replica_groups=mesh['case'=2,'tm'=4,'bundle'=2,'sub'=2] {'bundle'}, use_global_device_ids=true, to_apply=%region_3.4 | all-reduce | flops 1 | bytes 8 | tf_op jit(solution)/shard_map/psum | solution.py:161
  150.0 9.6 %psum.23 = f32[]{:T(128)} all-reduce(f32[]{:T(128)} %psum.22), channel_id=1, replica_groups=mesh['case'=2,'tm'=4,'bundle'=2,'sub'=2] {'tm'}, use_global_device_ids=true, to_apply=%region_4.5 | all-reduce | flops 1 | bytes 8 | tf_op jit(solution)/shard_map/psum | solution.py:161
  161.6 1.4 copy.26
  164.1 1.5 reshape.112
  (30 shorter events, 11.4 us)
Async XLA Ops:
  8.0 108.2 %all-gather.2.cloned.1.call-start = ((), (), s32[]{:S(2)}) async-start(), calls=%async_computation.4 | async-start | bytes 5242880 | tf_op jit(solution)/shard_map/all_gather | solution.py:119
  19.2 2.4 %copy-start = (bf16[2048,256]{1,0:T(8,128)(2,1)S(1)}, bf16[2048,256]{1,0:T(8,128)(2,1)}, u32[]{:S(2)}) copy-start(bf16[2048,256]{1,0:T(8,128)(2,1)} %param.5) | copy-start | bytes 3145732
  19.2 3.2 %copy-start.1 = (s32[4,64]{1,0:T(4,128)S(1)}, s32[4,64]{1,0:T(4,128)}, u32[]{:S(2)}) copy-start(s32[4,64]{1,0:T(4,128)} %param.8) | copy-start | bytes 3076
  21.5 140.1 %reduce-scatter.2.cloned.1.call-start = ((), (), s32[]{:S(2)}) async-start(), calls=%async_computation.3 | async-start | bytes 3145728 | tf_op jit(solution)/shard_map/reduce_scatter | solution.py:142
  24.2 25.9 %collective-permute-start = (bf16[4,32,256]{2,1,0:T(8,128)(2,1)S(1)}, bf16[4,32,256]{2,1,0:T(8,128)(2,1)S(1)}, u32[]{:S(2)}, u32[]{:S(2)}) collective-permute-start(bf16[4,32,256]{2,1,0:T(8,128)(2,1)S(1)} %slice.20), channel_id=1, source_target_pairs={{4,0},{8,4},{12,8},{5,1},{9,5},{13,9},{6,2},{10,6},{14,10},{7,3},{... | collective-permute-start | bytes 196616 | tf_op jit(solution)/shard_map/ppermute | solution.py:25
  63.2 36.9 %all-to-all-start = ((bf16[2,2048,4,16]{1,3,0,2:T(8,128)(2,1)}), bf16[2,2048,4,16]{1,3,0,2:T(8,128)(2,1)S(1)}, u32[]{:S(2)}, u32[]{:S(2)}) async-start(bf16[2,2048,4,16]{1,3,0,2:T(8,128)(2,1)} %copy.30), calls=%async_computation.1 | async-start | bytes 1048576 | tf_op jit(solution)/shard_map/all_to_all | solution.py:124
Sparse Core Ops, SparseCore 0:
  21.6 94.5 all-gather.1
Sparse Core Ops, SparseCore 1:
  60.7 13.2 reduce-scatter.1

commit v5 on v4

--- a/solution.py
+++ b/solution.py
@@ -121,7 +121,17 @@
     m16 = jnp.pad(m16, ((0, 0), (lag_steps - 1, 0), (0, 0))).astype(jnp.float32)
     reord_mine = lax.dynamic_slice_in_dim(r4.reshape(nb, seg_rows, width), sub * half, half, 0)
     r_split = reord_mine.reshape(half, seg_rows, n_tm, chunk)
-    r_all = lax.all_to_all(r_split, "tm", 2, 1, tiled=True)
+    tm_idx = lax.axis_index("tm")
+    own_piece = lax.dynamic_index_in_dim(r_split, tm_idx, 2, keepdims=False)
+    pieces = []
+    for e in range(-(n_tm - 1), n_tm):
+        if e == 0:
+            pieces.append(own_piece)
+            continue
+        wanted = lax.dynamic_index_in_dim(r_split, jnp.clip(tm_idx - e, 0, n_tm - 1), 2, keepdims=False)
+        pieces.append(passed_along(wanted, "tm", -e))
+    relative = jnp.concatenate(pieces, axis=1)
+    r_all = lax.dynamic_slice_in_dim(relative, (n_tm - 1 - tm_idx) * seg_rows, n_tm * seg_rows, 1)
     r16t = jnp.transpose(r_all.reshape(half, rows16, band, chunk), (0, 2, 3, 1)).reshape(half, band * chunk, rows16)
     acc_rows = (pad + lags_span(all_lags, band) + pad) * chunk
     raw_half = pl.pallas_call(

time: 174 us -> 174 us (level)
  starting transfers between devices: 8.68 us -> 23.4 us
  waiting for transfers between devices: 36.4 us -> 22.4 us
    all_to_all x1 -> x0, waiting for transfers between devices: 29.6 us -> none  [local(): r_all = lax.all_to_all(r_split, 'tm', 2, 1, tiled=True)]
    ppermute x1 -> x7, starting transfers between devices: 1.29 us -> 23.3 us  [passed_along(): return lax.ppermute(block, axis, route)]
    ppermute x1 -> x7, waiting for transfers between devices: 0.01 us -> 8.82 us  [passed_along(): return lax.ppermute(block, axis, route)]
    all_to_all x1 -> x0, starting transfers between devices: 7.31 us -> none  [local(): r_all = lax.all_to_all(r_split, 'tm', 2, 1, tiled=True)]
    all_gather x1, waiting for transfers between devices: 6.76 us -> 13.5 us  [local(): m_all = lax.all_gather(mine, 'tm', axis=1, tiled=True)]
  transfers between devices with their start and end apart: 4 -> 9, of which waited for: 2 -> 3; matrix products, arithmetic and copies ran while one was open for 32% -> 31% of each run, Pallas kernels for 10% -> 10%
where the time goes in v5:
time: 174 us; the launch traced here: 173 us
  local copies, waits for them, and re-layouts  47.8 us (27%)
  starting transfers between devices  23.4 us (13%)
  blocking collectives  22.8 us (13%)
  waiting for transfers between devices  22.4 us (13%)
  other arithmetic  21.4 us (12%)
  between operations  17.2 us (10%)
  Pallas kernels  16.9 us (10%)
    ppermute x7, starting transfers between devices, passed_along(): return lax.ppermute(block, axis, route)  23.3 us
    psum x3, blocking collectives, local(): total_squares = lax.psum(total_squares, axis)  18.2 us
    all_gather x1, waiting for transfers between devices, local(): m_all = lax.all_gather(mine, 'tm', axis=1, tiled=True)  13.5 us
    slice x1, local copies, waits for them, and re-layouts, local(): lax.slice_in_dim(kpad, tr - 1 - u, tr - 1 - u + stripes, 1, 1)  9.39 us
    ppermute x7, waiting for transfers between devices, passed_along(): return lax.ppermute(block, axis, route)  8.82 us
    pallas_call x1, Pallas kernels, local(): pl.pallas_call(functools.partial(dx_kernel, lag_tiles=lag_tiles, rows=row...  8.77 us
    concatenate x1, other arithmetic, local(): jnp.concatenate([lax.slice_in_dim(kpad, tr - 1 - u, tr - 1 - u + stripes,...  8.23 us
    pallas_call x1, Pallas kernels, local(): pl.pallas_call(functools.partial(raw_kernel, lag_steps=lag_steps, rows=ro...  8.15 us
  transfers between devices with their start and end apart: 9, of which 3 were waited for; matrix products, arithmetic and copies ran while one was open for 31% of the time, Pallas kernels for 10%

profile of v5, /device:TPU:0, one launch (start us, length us, event | category | flops | bytes accessed | tf_op | source)
XLA Modules:
  0.0 173.0 jit_solution(843937691893998060)
XLA Ops:
  8.7 3.3 %reshape.115 = bf16[512,4,4,64]{3,2,1,0:T(4,128)(2,1)S(1)} reshape(bf16[2048,256]{1,0:T(8,128)(2,1)} %param.6) | data formatting | bytes 2097152 | tf_op jit(solution)/shard_map/reshape | solution.py:86
  12.2 7.0 %broadcast_select_fusion = bf16[512,4,4,64]{3,2,1,0:T(4,128)(2,1)S(1)} fusion(bf16[512,4,4,64]{3,2,1,0:T(4,128)(2,1)S(1)} %reshape.115, pred[512,4]{1,0:T(8,128)(4,1)S(1)} %add_compare_fusion), kind=kLoop, calls=%fused_computation.8 | loop fusion | flops 524288 | bytes 2099200 | tf_op jit(solution)/shard_map/jit(_where)/select_n | solution.py:87
  25.5 6.9 %reshape.108 = bf16[4,64,64,64]{3,2,1,0:T(8,128)(2,1)} reshape(bf16[4,64,4096]{2,1,0:T(8,128)(2,1)} %param.7) | data formatting | bytes 4194304 | tf_op jit(solution)/shard_map/reshape | solution.py:92
  32.4 9.4 %pad_slice_fusion.3 = (bf16[4,68,64,64]{3,2,1,0:T(8,128)(2,1)S(1)}, bf16[4,68,64,64]{3,2,1,0:T(8,128)(2,1)S(1)}, bf16[4,68,64,64]{3,2,1,0:T(8,128)(2,1)S(1)}, bf16[4,68,64,64]{3,2,1,0:T(8,128)(2,1)S(1)}) fusion(bf16[4,64,64,64]{3,2,1,0:T(8,128)(2,1)} %reshape.108), kind=kLoop, calls=%fused_computation.4 | loop fusion | bytes 11010048 | tf_op jit(solution)/shard_map/slice | solution.py:96
  41.8 8.2 %pad_maximum_fusion = bf16[4,68,64,256]{3,2,1,0:T(8,128)(2,1)} fusion(bf16[4,68,64,64]{3,2,1,0:T(8,128)(2,1)S(1)} %get-tuple-element.5, bf16[4,68,64,64]{3,2,1,0:T(8,128)(2,1)S(1)} %get-tuple-element.4, bf16[4,68,64,64]{3,2,1,0:T(8,128)(2,1)S(1)} %get-tuple-element.3, bf16[4,68,64,64]{3,2,1,0:T(8,128)(2,1)S(1)} %get-tuple-element.2), kind=kLoop, calls=%fused_computation | loop fusion | flops 35651584 | bytes 17825792 | tf_op jit(solution)/shard_map/concatenate | solution.py:95
  50.0 1.7 fusion.6.r_ref
  51.8 8.8 %shard_map.68 = f32[4,512,256]{2,1,0:T(8,128)} custom-call(f32[4,528,256]{2,1,0:T(8,128)} %fusion.6.r_ref, bf16[4,4352,256]{2,1,0:T(8,128)(2,1)} %bitcast.44), custom_call_target="tpu_custom_call" | custom-call | tf_op jit(solution)/shard_map/pallas_call | solution.py:99
  62.5 7.9 %collective-permute-start.1 = (bf16[2,2048,16]{1,2,0:T(8,128)(2,1)S(1)}, bf16[2,2048,16]{1,2,0:T(8,128)(2,1)S(1)}, u32[]{:S(2)}, u32[]{:S(2)}) collective-permute-start(bf16[2,2048,16]{1,2,0:T(8,128)(2,1)S(1)} %get-tuple-element.11), channel_id=1, source_target_pairs={{0,12},{1,13},{2,14},{3,15},{16,28},{17,29},{18,30},{19,31}} | collective-permute-start | bytes 393224 | tf_op jit(solution)/shard_map/ppermute | solution.py:25
  74.3 4.7 %collective-permute-start.3 = (bf16[2,2048,16]{1,2,0:T(8,128)(2,1)S(1)}, bf16[2,2048,16]{1,2,0:T(8,128)(2,1)S(1)}, u32[]{:S(2)}, u32[]{:S(2)}) collective-permute-start(bf16[2,2048,16]{1,2,0:T(8,128)(2,1)S(1)} %get-tuple-element.9), channel_id=1, source_target_pairs={{0,4},{4,8},{8,12},{1,5},{5,9},{9,13},{2,6},{6,10},{10,14},{3,7},{... | collective-permute-start | bytes 393224 | tf_op jit(solution)/shard_map/ppermute | solution.py:25
  79.1 5.5 %collective-permute-start.2 = (bf16[2,2048,16]{1,2,0:T(8,128)(2,1)S(1)}, bf16[2,2048,16]{1,2,0:T(8,128)(2,1)S(1)}, u32[]{:S(2)}, u32[]{:S(2)}) collective-permute-start(bf16[2,2048,16]{1,2,0:T(8,128)(2,1)S(1)} %get-tuple-element.10), channel_id=1, source_target_pairs={{0,8},{4,12},{1,9},{5,13},{2,10},{6,14},{3,11},{7,15},{16,24},{20,... | collective-permute-start | bytes 393224 | tf_op jit(solution)/shard_map/ppermute | solution.py:25
  84.6 6.2 %collective-permute-done.2 = bf16[2,2048,16]{1,2,0:T(8,128)(2,1)S(1)} collective-permute-done((bf16[2,2048,16]{1,2,0:T(8,128)(2,1)S(1)}, bf16[2,2048,16]{1,2,0:T(8,128)(2,1)S(1)}, u32[]{:S(2)}, u32[]{:S(2)}) %collective-permute-start.2) | collective-permute-done | bytes 131104 | tf_op jit(solution)/shard_map/ppermute | solution.py:25
  90.9 2.6 %collective-permute-done.5 = bf16[2,2048,16]{1,2,0:T(8,128)(2,1)S(1)} collective-permute-done((bf16[2,2048,16]{1,2,0:T(8,128)(2,1)S(1)}, bf16[2,2048,16]{1,2,0:T(8,128)(2,1)S(1)}, u32[]{:S(2)}, u32[]{:S(2)}) %collective-permute-start.5) | collective-permute-done | bytes 131104 | tf_op jit(solution)/shard_map/ppermute | solution.py:25
  93.6 4.5 %reshape.113 = bf16[2,512,16,16]{2,1,3,0:T(8,128)(2,1)} reshape(bf16[2,8192,16]{1,2,0:T(8,128)(2,1)S(1)} %constant_dynamic-slice_fusion.1) | data formatting | bytes 1048576 | tf_op jit(solution)/shard_map/reshape | solution.py:135
  98.1 4.6 %copy.29 = bf16[2,16,16,512]{3,2,1,0:T(8,128)(2,1)} copy(bf16[2,16,16,512]{1,3,2,0:T(8,128)(2,1)} %bitcast.45) | data formatting | bytes 1048576 | tf_op jit(solution)/shard_map/transpose | solution.py:135
  102.7 13.5 %all-gather.2.cloned.1.call-done = bf16[2,8192,64]{2,1,0:T(8,128)(2,1)} async-done(((bf16[2,2048,64]{2,1,0:T(8,128)(2,1)}), bf16[2,8192,64]{2,1,0:T(8,128)(2,1)}) %all-gather.2.cloned.1.call-update) | async-done | bytes 2097168 | tf_op jit(solution)/shard_map/all_gather | solution.py:119
  116.2 5.5 %reshape.116 = bf16[2,512,1024]{2,1,0:T(8,128)(2,1)S(1)} reshape(bf16[2,8192,64]{2,1,0:T(8,128)(2,1)} %all-gather.2.cloned.1.call-done) | data formatting | bytes 4194304 | tf_op jit(solution)/shard_map/reshape | solution.py:120
  121.6 2.4 %pad_convert_fusion.m_ref = f32[2,520,1024]{2,1,0:T(8,128)} fusion(bf16[2,512,1024]{2,1,0:T(8,128)(2,1)S(1)} %reshape.116), kind=kLoop, calls=%fused_computation.5 | loop fusion | flops 1064960 | bytes 6356992 | tf_op jit(solution)/shard_map/convert_element_type | solution.py:121
  124.1 8.1 %shard_map.69 = f32[2,2048,64]{2,1,0:T(8,128)} custom-call(bf16[2,256,512]{2,1,0:T(8,128)(2,1)} %bitcast.55, f32[2,520,1024]{2,1,0:T(8,128)} %pad_convert_fusion.m_ref), custom_call_target="tpu_custom_call" | custom-call | tf_op jit(solution)/shard_map/pallas_call | solution.py:137
  132.2 2.0 %reshape.117 = f32[2,128,1024]{2,1,0:T(8,128)S(1)} reshape(f32[2,2048,64]{2,1,0:T(8,128)} %shard_map.69) | data formatting | bytes 2097152 | tf_op jit(solution)/shard_map/reshape | solution.py:149
  135.0 4.6 %all_to_all.4 = f32[2,128,1024]{2,0,1:T(2,128)S(1)} all-to-all(f32[2,128,1024]{2,0,1:T(2,128)S(1)} %copy.31), channel_id=1, replica_groups=mesh['case'=2,'tm'=4,'bundle'=2,'sub'=2] {'sub'}, dimensions={1} | all-to-all | bytes 2097152 | tf_op jit(solution)/shard_map/all_to_all | solution.py:150
  139.6 1.7 multiply_reduce_fusion
  141.3 3.1 %psum.21 = f32[]{:T(128)} all-reduce(f32[]{:T(128)} %multiply_reduce_fusion), channel_id=1, replica_groups=mesh['case'=2,'tm'=4,'bundle'=2,'sub'=2] {'sub'}, use_global_device_ids=true, to_apply=%region_2.3 | all-reduce | flops 1 | bytes 8 | tf_op jit(solution)/shard_map/psum | solution.py:171
  144.4 5.5 %psum.22 = f32[]{:T(128)} all-reduce(f32[]{:T(128)} %psum.21), channel_id=1, replica_groups=mesh['case'=2,'tm'=4,'bundle'=2,'sub'=2] {'bundle'}, use_global_device_ids=true, to_apply=%region_3.4 | all-reduce | flops 1 | bytes 8 | tf_op jit(solution)/shard_map/psum | solution.py:171
  149.9 9.6 %psum.23 = f32[]{:T(128)} all-reduce(f32[]{:T(128)} %psum.22), channel_id=1, replica_groups=mesh['case'=2,'tm'=4,'bundle'=2,'sub'=2] {'tm'}, use_global_device_ids=true, to_apply=%region_4.5 | all-reduce | flops 1 | bytes 8 | tf_op jit(solution)/shard_map/psum | solution.py:171
  (47 shorter events, 18.5 us)
Async XLA Ops:
  8.0 108.2 %all-gather.2.cloned.1.call-start = ((), (), s32[]{:S(2)}) async-start(), calls=%async_computation.3 | async-start | bytes 5242880 | tf_op jit(solution)/shard_map/all_gather | solution.py:119
  19.2 2.4 %copy-start = (bf16[2048,256]{1,0:T(8,128)(2,1)S(1)}, bf16[2048,256]{1,0:T(8,128)(2,1)}, u32[]{:S(2)}) copy-start(bf16[2048,256]{1,0:T(8,128)(2,1)} %param.5) | copy-start | bytes 3145732
  19.2 3.2 %copy-start.1 = (s32[4,64]{1,0:T(4,128)S(1)}, s32[4,64]{1,0:T(4,128)}, u32[]{:S(2)}) copy-start(s32[4,64]{1,0:T(4,128)} %param.8) | copy-start | bytes 3076
  21.5 140.1 %reduce-scatter.2.cloned.1.call-start = ((), (), s32[]{:S(2)}) async-start(), calls=%async_computation.2 | async-start | bytes 3145728 | tf_op jit(solution)/shard_map/reduce_scatter | solution.py:152
  24.2 25.8 %collective-permute-start = (bf16[4,32,256]{2,1,0:T(8,128)(2,1)S(1)}, bf16[4,32,256]{2,1,0:T(8,128)(2,1)S(1)}, u32[]{:S(2)}, u32[]{:S(2)}) collective-permute-start(bf16[4,32,256]{2,1,0:T(8,128)(2,1)S(1)} %slice.20), channel_id=1, source_target_pairs={{4,0},{8,4},{12,8},{5,1},{9,5},{13,9},{6,2},{10,6},{14,10},{7,3},{... | collective-permute-start | bytes 196616 | tf_op jit(solution)/shard_map/ppermute | solution.py:25
  62.5 16.6 %collective-permute-start.1 = (bf16[2,2048,16]{1,2,0:T(8,128)(2,1)S(1)}, bf16[2,2048,16]{1,2,0:T(8,128)(2,1)S(1)}, u32[]{:S(2)}, u32[]{:S(2)}) collective-permute-start(bf16[2,2048,16]{1,2,0:T(8,128)(2,1)S(1)} %get-tuple-element.11), channel_id=1, source_target_pairs={{0,12},{1,13},{2,14},{3,15},{16,28},{17,29},{18,30},{19,31}} | collective-permute-start | bytes 393224 | tf_op jit(solution)/shard_map/ppermute | solution.py:25
  70.4 23.1 %collective-permute-start.6 = (bf16[2,2048,16]{1,2,0:T(8,128)(2,1)S(1)}, bf16[2,2048,16]{1,2,0:T(8,128)(2,1)S(1)}, u32[]{:S(2)}, u32[]{:S(2)}) collective-permute-start(bf16[2,2048,16]{1,2,0:T(8,128)(2,1)S(1)} %get-tuple-element.6), channel_id=1, source_target_pairs={{12,0},{13,1},{14,2},{15,3},{28,16},{29,17},{30,18},{31,19}} | collective-permute-start | bytes 393224 | tf_op jit(solution)/shard_map/ppermute | solution.py:25
  71.7 21.7 %collective-permute-start.5 = (bf16[2,2048,16]{1,2,0:T(8,128)(2,1)S(1)}, bf16[2,2048,16]{1,2,0:T(8,128)(2,1)S(1)}, u32[]{:S(2)}, u32[]{:S(2)}) collective-permute-start(bf16[2,2048,16]{1,2,0:T(8,128)(2,1)S(1)} %get-tuple-element.7), channel_id=1, source_target_pairs={{8,0},{12,4},{9,1},{13,5},{10,2},{14,6},{11,3},{15,7},{24,16},{28,... | collective-permute-start | bytes 393224 | tf_op jit(solution)/shard_map/ppermute | solution.py:25
  73.0 17.8 %collective-permute-start.4 = (bf16[2,2048,16]{1,2,0:T(8,128)(2,1)S(1)}, bf16[2,2048,16]{1,2,0:T(8,128)(2,1)S(1)}, u32[]{:S(2)}, u32[]{:S(2)}) collective-permute-start(bf16[2,2048,16]{1,2,0:T(8,128)(2,1)S(1)} %get-tuple-element.8), channel_id=1, source_target_pairs={{4,0},{8,4},{12,8},{5,1},{9,5},{13,9},{6,2},{10,6},{14,10},{7,3},{... | collective-permute-start | bytes 393224 | tf_op jit(solution)/shard_map/ppermute | solution.py:25
  74.3 16.4 %collective-permute-start.3 = (bf16[2,2048,16]{1,2,0:T(8,128)(2,1)S(1)}, bf16[2,2048,16]{1,2,0:T(8,128)(2,1)S(1)}, u32[]{:S(2)}, u32[]{:S(2)}) collective-permute-start(bf16[2,2048,16]{1,2,0:T(8,128)(2,1)S(1)} %get-tuple-element.9), channel_id=1, source_target_pairs={{0,4},{4,8},{8,12},{1,5},{5,9},{9,13},{2,6},{6,10},{10,14},{3,7},{... | collective-permute-start | bytes 393224 | tf_op jit(solution)/shard_map/ppermute | solution.py:25
  79.1 11.7 %collective-permute-start.2 = (bf16[2,2048,16]{1,2,0:T(8,128)(2,1)S(1)}, bf16[2,2048,16]{1,2,0:T(8,128)(2,1)S(1)}, u32[]{:S(2)}, u32[]{:S(2)}) collective-permute-start(bf16[2,2048,16]{1,2,0:T(8,128)(2,1)S(1)} %get-tuple-element.10), channel_id=1, source_target_pairs={{0,8},{4,12},{1,9},{5,13},{2,10},{6,14},{3,11},{7,15},{16,24},{20,... | collective-permute-start | bytes 393224 | tf_op jit(solution)/shard_map/ppermute | solution.py:25
Sparse Core Ops, SparseCore 0:
  21.6 94.5 all-gather.1
Sparse Core Ops, SparseCore 1:
  60.6 13.2 reduce-scatter.1

commit v6 on v5

--- a/solution.py
+++ b/solution.py
@@ -116,7 +116,11 @@
     lag_steps = all_lags // band + 1
     pad = band
     mine = lax.dynamic_slice_in_dim(m4.reshape(nb, seg_rows, width), sub * half, half, 0)
-    m_all = lax.all_gather(mine, "tm", axis=1, tiled=True)
+    m_pieces = []
+    for e in range(-(n_tm - 1), n_tm):
+        m_pieces.append(mine if e == 0 else passed_along(mine, "tm", -e))
+    m_relative = jnp.concatenate(m_pieces, axis=1)
+    m_all = lax.dynamic_slice_in_dim(m_relative, (n_tm - 1 - lax.axis_index("tm")) * seg_rows, n_tm * seg_rows, 1)
     m16 = m_all.reshape(half, rows16, band * width)
     m16 = jnp.pad(m16, ((0, 0), (lag_steps - 1, 0), (0, 0))).astype(jnp.float32)
     reord_mine = lax.dynamic_slice_in_dim(r4.reshape(nb, seg_rows, width), sub * half, half, 0)

time: 174 us -> 202 us (1.16)
  local copies, waits for them, and re-layouts: 47.8 us -> 60 us
  waiting for transfers between devices: 22.4 us -> 31.4 us
  starting transfers between devices: 23.4 us -> 31.6 us
    ppermute x7 -> x13, waiting for transfers between devices: 8.82 us -> 31.4 us  [passed_along(): return lax.ppermute(block, axis, route)]
    all_gather x1 -> x0, waiting for transfers between devices: 13.5 us -> none  [local(): m_all = lax.all_gather(mine, 'tm', axis=1, tiled=True)]
    ppermute x7 -> x13, starting transfers between devices: 23.3 us -> 31.6 us  [passed_along(): return lax.ppermute(block, axis, route)]
    unnamed x11 -> x19, local copies, waits for them, and re-layouts: 1.19 us -> 6.34 us
    dynamic_slice x0 -> x2, local copies, waits for them, and re-layouts: none -> 3.36 us  [local(): lax.dynamic_slice_in_dim(m_relative, (n_tm - 1 - lax.axis_index('tm')) *...]
    reshape x1, local copies, waits for them, and re-layouts: 0.86 us -> 3.32 us  [local(): cot4 = cotangent.reshape(rows4, tr, nb, width)]
  transfers between devices with their start and end apart: 9 -> 14, of which waited for: 3 -> 6; matrix products, arithmetic and copies ran while one was open for 31% -> 33% of each run, Pallas kernels for 10% -> 8%
where the time goes in v6:
time: 202 us; the launch traced here: 201 us
  local copies, waits for them, and re-layouts  60 us (30%)
  starting transfers between devices  31.6 us (16%)
  waiting for transfers between devices  31.4 us (16%)
  blocking collectives  22.2 us (11%)
  other arithmetic  21.4 us (11%)
  Pallas kernels  16.9 us (8%)
  between operations  15.9 us (8%)
    ppermute x13, starting transfers between devices, passed_along(): return lax.ppermute(block, axis, route)  31.6 us
    ppermute x13, waiting for transfers between devices, passed_along(): return lax.ppermute(block, axis, route)  31.4 us
    psum x3, blocking collectives, local(): total_squares = lax.psum(total_squares, axis)  17.6 us
    slice x1, local copies, waits for them, and re-layouts, local(): lax.slice_in_dim(kpad, tr - 1 - u, tr - 1 - u + stripes, 1, 1)  9.53 us
    pallas_call x1, Pallas kernels, local(): pl.pallas_call(functools.partial(dx_kernel, lag_tiles=lag_tiles, rows=row...  8.74 us
    concatenate x1, other arithmetic, local(): jnp.concatenate([lax.slice_in_dim(kpad, tr - 1 - u, tr - 1 - u + stripes,...  8.23 us
    pallas_call x1, Pallas kernels, local(): pl.pallas_call(functools.partial(raw_kernel, lag_steps=lag_steps, rows=ro...  8.15 us
    select_n x1, other arithmetic, local(): jnp.where(live4[None, :, :, None], inp4, jnp.zeros((), jnp.bfloat16))  6.98 us
  transfers between devices with their start and end apart: 14, of which 6 were waited for; matrix products, arithmetic and copies ran while one was open for 33% of the time, Pallas kernels for 8%

profile of v6, /device:TPU:0, one launch (start us, length us, event | category | flops | bytes accessed | tf_op | source)
XLA Modules:
  0.0 200.6 jit_solution(7254915399765799073)
XLA Ops:
  7.9 3.3 %reshape.115 = bf16[512,4,4,64]{3,2,1,0:T(4,128)(2,1)S(1)} reshape(bf16[2048,256]{1,0:T(8,128)(2,1)} %param.6) | data formatting | bytes 2097152 | tf_op jit(solution)/shard_map/reshape | solution.py:86
  11.3 7.0 %broadcast_select_fusion = bf16[512,4,4,64]{3,2,1,0:T(4,128)(2,1)S(1)} fusion(bf16[512,4,4,64]{3,2,1,0:T(4,128)(2,1)S(1)} %reshape.115, pred[512,4]{1,0:T(8,128)(4,1)S(1)} %add_compare_fusion), kind=kLoop, calls=%fused_computation.8 | loop fusion | flops 524288 | bytes 2099200 | tf_op jit(solution)/shard_map/jit(_where)/select_n | solution.py:87
  24.0 5.9 %collective-permute-start.9 = (bf16[2,2048,64]{1,2,0:T(8,128)(2,1)}, bf16[2,2048,64]{1,2,0:T(8,128)(2,1)}, u32[]{:S(2)}, u32[]{:S(2)}) collective-permute-start(bf16[2,2048,64]{1,2,0:T(8,128)(2,1)} %copy.35), channel_id=1, source_target_pairs={{0,4},{4,8},{8,12},{1,5},{5,9},{9,13},{2,6},{6,10},{10,14},{3,7},{... | collective-permute-start | bytes 1572872 | tf_op jit(solution)/shard_map/ppermute | solution.py:25
  29.9 6.2 %collective-permute-start.8 = (bf16[2,2048,64]{1,2,0:T(8,128)(2,1)}, bf16[2,2048,64]{1,2,0:T(8,128)(2,1)}, u32[]{:S(2)}, u32[]{:S(2)}) collective-permute-start(bf16[2,2048,64]{1,2,0:T(8,128)(2,1)} %copy.35), channel_id=1, source_target_pairs={{0,8},{4,12},{1,9},{5,13},{2,10},{6,14},{3,11},{7,15},{16,24},{20,... | collective-permute-start | bytes 1572872 | tf_op jit(solution)/shard_map/ppermute | solution.py:25
  36.1 3.3 %reshape.106 = bf16[512,4,4,64]{3,2,1,0:T(4,128)(2,1)S(1)} reshape(bf16[2048,256]{1,0:T(8,128)(2,1)} %param.5) | data formatting | bytes 2097152 | tf_op jit(solution)/shard_map/reshape | solution.py:77
  44.4 6.9 %reshape.108 = bf16[4,64,64,64]{3,2,1,0:T(8,128)(2,1)} reshape(bf16[4,64,4096]{2,1,0:T(8,128)(2,1)} %param.7) | data formatting | bytes 4194304 | tf_op jit(solution)/shard_map/reshape | solution.py:92
  51.3 9.5 %pad_slice_fusion.3 = (bf16[4,68,64,64]{3,2,1,0:T(8,128)(2,1)S(1)}, bf16[4,68,64,64]{3,2,1,0:T(8,128)(2,1)S(1)}, bf16[4,68,64,64]{3,2,1,0:T(8,128)(2,1)S(1)}, bf16[4,68,64,64]{3,2,1,0:T(8,128)(2,1)S(1)}) fusion(bf16[4,64,64,64]{3,2,1,0:T(8,128)(2,1)} %reshape.108), kind=kLoop, calls=%fused_computation.4 | loop fusion | bytes 11010048 | tf_op jit(solution)/shard_map/slice | solution.py:96
  60.9 8.2 %pad_maximum_fusion = bf16[4,68,64,256]{3,2,1,0:T(8,128)(2,1)} fusion(bf16[4,68,64,64]{3,2,1,0:T(8,128)(2,1)S(1)} %get-tuple-element.5, bf16[4,68,64,64]{3,2,1,0:T(8,128)(2,1)S(1)} %get-tuple-element.4, bf16[4,68,64,64]{3,2,1,0:T(8,128)(2,1)S(1)} %get-tuple-element.3, bf16[4,68,64,64]{3,2,1,0:T(8,128)(2,1)S(1)} %get-tuple-element.2), kind=kLoop, calls=%fused_computation | loop fusion | flops 35651584 | bytes 17825792 | tf_op jit(solution)/shard_map/concatenate | solution.py:95
  69.2 2.8 %collective-permute-start.1 = (bf16[2,2048,16]{1,2,0:T(8,128)(2,1)S(1)}, bf16[2,2048,16]{1,2,0:T(8,128)(2,1)S(1)}, u32[]{:S(2)}, u32[]{:S(2)}) collective-permute-start(bf16[2,2048,16]{1,2,0:T(8,128)(2,1)S(1)} %get-tuple-element.11), channel_id=1, source_target_pairs={{0,12},{1,13},{2,14},{3,15},{16,28},{17,29},{18,30},{19,31}} | collective-permute-start | bytes 393224 | tf_op jit(solution)/shard_map/ppermute | solution.py:25
  73.8 8.7 %shard_map.68 = f32[4,512,256]{2,1,0:T(8,128)} custom-call(f32[4,528,256]{2,1,0:T(8,128)} %fusion.6.r_ref, bf16[4,4352,256]{2,1,0:T(8,128)(2,1)} %bitcast.44), custom_call_target="tpu_custom_call" | custom-call | tf_op jit(solution)/shard_map/pallas_call | solution.py:99
  86.6 4.7 %collective-permute-start.3 = (bf16[2,2048,16]{1,2,0:T(8,128)(2,1)S(1)}, bf16[2,2048,16]{1,2,0:T(8,128)(2,1)S(1)}, u32[]{:S(2)}, u32[]{:S(2)}) collective-permute-start(bf16[2,2048,16]{1,2,0:T(8,128)(2,1)S(1)} %get-tuple-element.9), channel_id=1, source_target_pairs={{0,4},{4,8},{8,12},{1,5},{5,9},{9,13},{2,6},{6,10},{10,14},{3,7},{... | collective-permute-start | bytes 393224 | tf_op jit(solution)/shard_map/ppermute | solution.py:25
  95.1 5.9 %collective-permute-done.4 = bf16[2,2048,16]{1,2,0:T(8,128)(2,1)S(1)} collective-permute-done((bf16[2,2048,16]{1,2,0:T(8,128)(2,1)S(1)}, bf16[2,2048,16]{1,2,0:T(8,128)(2,1)S(1)}, u32[]{:S(2)}, u32[]{:S(2)}) %collective-permute-start.4) | collective-permute-done | bytes 131104 | tf_op jit(solution)/shard_map/ppermute | solution.py:25
  102.3 6.4 %collective-permute-done.5 = bf16[2,2048,16]{1,2,0:T(8,128)(2,1)S(1)} collective-permute-done((bf16[2,2048,16]{1,2,0:T(8,128)(2,1)S(1)}, bf16[2,2048,16]{1,2,0:T(8,128)(2,1)S(1)}, u32[]{:S(2)}, u32[]{:S(2)}) %collective-permute-start.5) | collective-permute-done | bytes 131104 | tf_op jit(solution)/shard_map/ppermute | solution.py:25
  110.1 7.3 %collective-permute-done.6 = bf16[2,2048,16]{1,2,0:T(8,128)(2,1)S(1)} collective-permute-done((bf16[2,2048,16]{1,2,0:T(8,128)(2,1)S(1)}, bf16[2,2048,16]{1,2,0:T(8,128)(2,1)S(1)}, u32[]{:S(2)}, u32[]{:S(2)}) %collective-permute-start.6) | collective-permute-done | bytes 131104 | tf_op jit(solution)/shard_map/ppermute | solution.py:25
  119.0 4.6 %reshape.113 = bf16[2,512,16,16]{2,1,3,0:T(8,128)(2,1)} reshape(bf16[2,8192,16]{1,2,0:T(8,128)(2,1)S(1)} %constant_dynamic-slice_fusion.2) | data formatting | bytes 1048576 | tf_op jit(solution)/shard_map/reshape | solution.py:139
  123.5 4.6 %copy.29 = bf16[2,16,16,512]{3,2,1,0:T(8,128)(2,1)} copy(bf16[2,16,16,512]{1,3,2,0:T(8,128)(2,1)} %bitcast.45) | data formatting | bytes 1048576 | tf_op jit(solution)/shard_map/transpose | solution.py:139
  132.7 6.7 %collective-permute-done.10 = bf16[2,2048,64]{1,2,0:T(8,128)(2,1)S(1)} collective-permute-done((bf16[2,2048,64]{1,2,0:T(8,128)(2,1)}, bf16[2,2048,64]{1,2,0:T(8,128)(2,1)S(1)}, u32[]{:S(2)}, u32[]{:S(2)}) %collective-permute-start.10) | collective-permute-done | bytes 524320 | tf_op jit(solution)/shard_map/ppermute | solution.py:25
  141.8 3.2 %copy.31 = bf16[2,8192,64]{2,1,0:T(8,128)(2,1)} copy(bf16[2,8192,64]{1,2,0:T(8,128)(2,1)S(1)} %constant_dynamic-slice_fusion) | data formatting | bytes 4194304 | tf_op jit(solution)/shard_map/dynamic_slice | solution.py:123
  145.0 5.5 %reshape.116 = bf16[2,512,1024]{2,1,0:T(8,128)(2,1)S(1)} reshape(bf16[2,8192,64]{2,1,0:T(8,128)(2,1)} %copy.31) | data formatting | bytes 4194304 | tf_op jit(solution)/shard_map/reshape | solution.py:124
  152.9 8.2 %shard_map.69 = f32[2,2048,64]{2,1,0:T(8,128)} custom-call(bf16[2,256,512]{2,1,0:T(8,128)(2,1)} %bitcast.55, f32[2,520,1024]{2,1,0:T(8,128)} %pad_convert_fusion.m_ref), custom_call_target="tpu_custom_call" | custom-call | tf_op jit(solution)/shard_map/pallas_call | solution.py:141
  163.9 4.6 %all_to_all.4 = f32[2,128,1024]{2,0,1:T(2,128)S(1)} all-to-all(f32[2,128,1024]{2,0,1:T(2,128)S(1)} %copy.32), channel_id=1, replica_groups=mesh['case'=2,'tm'=4,'bundle'=2,'sub'=2] {'sub'}, dimensions={1} | all-to-all | bytes 2097152 | tf_op jit(solution)/shard_map/all_to_all | solution.py:154
  170.1 3.1 %psum.21 = f32[]{:T(128)} all-reduce(f32[]{:T(128)} %multiply_reduce_fusion), channel_id=1, replica_groups=mesh['case'=2,'tm'=4,'bundle'=2,'sub'=2] {'sub'}, use_global_device_ids=true, to_apply=%region_2.3 | all-reduce | flops 1 | bytes 8 | tf_op jit(solution)/shard_map/psum | solution.py:175
  173.2 5.5 %psum.22 = f32[]{:T(128)} all-reduce(f32[]{:T(128)} %psum.21), channel_id=1, replica_groups=mesh['case'=2,'tm'=4,'bundle'=2,'sub'=2] {'bundle'}, use_global_device_ids=true, to_apply=%region_3.4 | all-reduce | flops 1 | bytes 8 | tf_op jit(solution)/shard_map/psum | solution.py:175
  178.8 9.0 %psum.23 = f32[]{:T(128)} all-reduce(f32[]{:T(128)} %psum.22), channel_id=1, replica_groups=mesh['case'=2,'tm'=4,'bundle'=2,'sub'=2] {'tm'}, use_global_device_ids=true, to_apply=%region_4.5 | all-reduce | flops 1 | bytes 8 | tf_op jit(solution)/shard_map/psum | solution.py:175
  (67 shorter events, 43.6 us)
Async XLA Ops:
  7.2 182.6 %reduce-scatter.2.cloned.1.call-start = ((), (), s32[]{:S(2)}) async-start(), calls=%async_computation.2 | async-start | bytes 3145728 | tf_op jit(solution)/shard_map/reduce_scatter | solution.py:156
  18.3 21.1 %copy-start.2 = (s32[4,64]{1,0:T(4,128)S(1)}, s32[4,64]{1,0:T(4,128)}, u32[]{:S(2)}) copy-start(s32[4,64]{1,0:T(4,128)} %param.8) | copy-start | bytes 3076
  21.4 119.1 %collective-permute-start.12 = (bf16[2,2048,64]{1,2,0:T(8,128)(2,1)}, bf16[2,2048,64]{1,2,0:T(8,128)(2,1)}, u32[]{:S(2)}, u32[]{:S(2)}) collective-permute-start(bf16[2,2048,64]{1,2,0:T(8,128)(2,1)} %copy.35), channel_id=1, source_target_pairs={{12,0},{13,1},{14,2},{15,3},{28,16},{29,17},{30,18},{31,19}} | collective-permute-start | bytes 1572872 | tf_op jit(solution)/shard_map/ppermute | solution.py:25
  22.7 116.8 %collective-permute-start.11 = (bf16[2,2048,64]{1,2,0:T(8,128)(2,1)}, bf16[2,2048,64]{1,2,0:T(8,128)(2,1)}, u32[]{:S(2)}, u32[]{:S(2)}) collective-permute-start(bf16[2,2048,64]{1,2,0:T(8,128)(2,1)} %copy.35), channel_id=1, source_target_pairs={{8,0},{12,4},{9,1},{13,5},{10,2},{14,6},{11,3},{15,7},{24,16},{28,... | collective-permute-start | bytes 1572872 | tf_op jit(solution)/shard_map/ppermute | solution.py:25
  24.0 106.6 %collective-permute-start.9 = (bf16[2,2048,64]{1,2,0:T(8,128)(2,1)}, bf16[2,2048,64]{1,2,0:T(8,128)(2,1)}, u32[]{:S(2)}, u32[]{:S(2)}) collective-permute-start(bf16[2,2048,64]{1,2,0:T(8,128)(2,1)} %copy.35), channel_id=1, source_target_pairs={{0,4},{4,8},{8,12},{1,5},{5,9},{9,13},{2,6},{6,10},{10,14},{3,7},{... | collective-permute-start | bytes 1572872 | tf_op jit(solution)/shard_map/ppermute | solution.py:25
  29.9 99.5 %collective-permute-start.8 = (bf16[2,2048,64]{1,2,0:T(8,128)(2,1)}, bf16[2,2048,64]{1,2,0:T(8,128)(2,1)}, u32[]{:S(2)}, u32[]{:S(2)}) collective-permute-start(bf16[2,2048,64]{1,2,0:T(8,128)(2,1)} %copy.35), channel_id=1, source_target_pairs={{0,8},{4,12},{1,9},{5,13},{2,10},{6,14},{3,11},{7,15},{16,24},{20,... | collective-permute-start | bytes 1572872 | tf_op jit(solution)/shard_map/ppermute | solution.py:25
  41.3 1.4 copy-start
  41.3 27.9 %collective-permute-start = (bf16[4,32,256]{2,1,0:T(8,128)(2,1)S(1)}, bf16[4,32,256]{2,1,0:T(8,128)(2,1)S(1)}, u32[]{:S(2)}, u32[]{:S(2)}) collective-permute-start(bf16[4,32,256]{2,1,0:T(8,128)(2,1)S(1)} %slice.20), channel_id=1, source_target_pairs={{4,0},{8,4},{12,8},{5,1},{9,5},{13,9},{6,2},{10,6},{14,10},{7,3},{... | collective-permute-start | bytes 196616 | tf_op jit(solution)/shard_map/ppermute | solution.py:25
  60.9 11.1 %copy-start.1 = (bf16[4,512,256]{2,1,0:T(8,128)(2,1)S(1)}, bf16[4,512,256]{2,1,0:T(8,128)(2,1)}, u32[]{:S(2)}) copy-start(bf16[4,512,256]{2,1,0:T(8,128)(2,1)} %copy-done) | copy-start | bytes 3145732
  69.2 13.4 %collective-permute-start.1 = (bf16[2,2048,16]{1,2,0:T(8,128)(2,1)S(1)}, bf16[2,2048,16]{1,2,0:T(8,128)(2,1)S(1)}, u32[]{:S(2)}, u32[]{:S(2)}) collective-permute-start(bf16[2,2048,16]{1,2,0:T(8,128)(2,1)S(1)} %get-tuple-element.11), channel_id=1, source_target_pairs={{0,12},{1,13},{2,14},{3,15},{16,28},{17,29},{18,30},{19,31}} | collective-permute-start | bytes 393224 | tf_op jit(solution)/shard_map/ppermute | solution.py:25
  82.6 4.0 %collective-permute-start.2 = (bf16[2,2048,16]{1,2,0:T(8,128)(2,1)S(1)}, bf16[2,2048,16]{1,2,0:T(8,128)(2,1)S(1)}, u32[]{:S(2)}, u32[]{:S(2)}) collective-permute-start(bf16[2,2048,16]{1,2,0:T(8,128)(2,1)S(1)} %get-tuple-element.10), channel_id=1, source_target_pairs={{0,8},{4,12},{1,9},{5,13},{2,10},{6,14},{3,11},{7,15},{16,24},{20,... | collective-permute-start | bytes 393224 | tf_op jit(solution)/shard_map/ppermute | solution.py:25
  86.6 7.2 %collective-permute-start.3 = (bf16[2,2048,16]{1,2,0:T(8,128)(2,1)S(1)}, bf16[2,2048,16]{1,2,0:T(8,128)(2,1)S(1)}, u32[]{:S(2)}, u32[]{:S(2)}) collective-permute-start(bf16[2,2048,16]{1,2,0:T(8,128)(2,1)S(1)} %get-tuple-element.9), channel_id=1, source_target_pairs={{0,4},{4,8},{8,12},{1,5},{5,9},{9,13},{2,6},{6,10},{10,14},{3,7},{... | collective-permute-start | bytes 393224 | tf_op jit(solution)/shard_map/ppermute | solution.py:25
  93.7 7.3 %collective-permute-start.4 = (bf16[2,2048,16]{1,2,0:T(8,128)(2,1)S(1)}, bf16[2,2048,16]{1,2,0:T(8,128)(2,1)S(1)}, u32[]{:S(2)}, u32[]{:S(2)}) collective-permute-start(bf16[2,2048,16]{1,2,0:T(8,128)(2,1)S(1)} %get-tuple-element.8), channel_id=1, source_target_pairs={{4,0},{8,4},{12,8},{5,1},{9,5},{13,9},{6,2},{10,6},{14,10},{7,3},{... | collective-permute-start | bytes 393224 | tf_op jit(solution)/shard_map/ppermute | solution.py:25
  101.0 7.7 %collective-permute-start.5 = (bf16[2,2048,16]{1,2,0:T(8,128)(2,1)S(1)}, bf16[2,2048,16]{1,2,0:T(8,128)(2,1)S(1)}, u32[]{:S(2)}, u32[]{:S(2)}) collective-permute-start(bf16[2,2048,16]{1,2,0:T(8,128)(2,1)S(1)} %get-tuple-element.7), channel_id=1, source_target_pairs={{8,0},{12,4},{9,1},{13,5},{10,2},{14,6},{11,3},{15,7},{24,16},{28,... | collective-permute-start | bytes 393224 | tf_op jit(solution)/shard_map/ppermute | solution.py:25
  108.8 8.6 %collective-permute-start.6 = (bf16[2,2048,16]{1,2,0:T(8,128)(2,1)S(1)}, bf16[2,2048,16]{1,2,0:T(8,128)(2,1)S(1)}, u32[]{:S(2)}, u32[]{:S(2)}) collective-permute-start(bf16[2,2048,16]{1,2,0:T(8,128)(2,1)S(1)} %get-tuple-element.6), channel_id=1, source_target_pairs={{12,0},{13,1},{14,2},{15,3},{28,16},{29,17},{30,18},{31,19}} | collective-permute-start | bytes 393224 | tf_op jit(solution)/shard_map/ppermute | solution.py:25
  117.4 10.7 %collective-permute-start.7 = (bf16[2,2048,64]{1,2,0:T(8,128)(2,1)}, bf16[2,2048,64]{1,2,0:T(8,128)(2,1)S(1)}, u32[]{:S(2)}, u32[]{:S(2)}) collective-permute-start(bf16[2,2048,64]{1,2,0:T(8,128)(2,1)} %copy.35), channel_id=1, source_target_pairs={{0,12},{1,13},{2,14},{3,15},{16,28},{17,29},{18,30},{19,31}} | collective-permute-start | bytes 1572872 | tf_op jit(solution)/shard_map/ppermute | solution.py:25
  128.1 11.3 %collective-permute-start.10 = (bf16[2,2048,64]{1,2,0:T(8,128)(2,1)}, bf16[2,2048,64]{1,2,0:T(8,128)(2,1)S(1)}, u32[]{:S(2)}, u32[]{:S(2)}) collective-permute-start(bf16[2,2048,64]{1,2,0:T(8,128)(2,1)} %copy.35), channel_id=1, source_target_pairs={{4,0},{8,4},{12,8},{5,1},{9,5},{13,9},{6,2},{10,6},{14,10},{7,3},{... | collective-permute-start | bytes 1572872 | tf_op jit(solution)/shard_map/ppermute | solution.py:25
Sparse Core Ops, SparseCore 0:
  82.7 8.5 reduce-scatter.1
